TPU v7x, 512 devices: a whole 4x8x8 slice. The times are simulated.
512 devices in a mesh: col: 8 (over z), tile: 64 (over y, x, core).
Axes of the slice: x: 4, y: 8, z: 8, core: 2. Of those that a mesh axis runs over, the one named last changes fastest.
Arguments:
- panel_factor: bfloat16 [8, 64, 2, 512, 512], P('col', 'tile'), may hold values from -0.15625 to 0.15625
- panel_cotangent: bfloat16 [8, 64, 2, 512, 512], P('col', 'tile'), may hold values from -1.5 to 1.5
- diag_factor: bfloat16 [8, 512, 512], P('col'), as said below
- diag_inverse: bfloat16 [8, 512, 512], P('col'), as said below
- diag_cotangent: float32 [8, 512, 512], P('col', 'tile'), may hold values from -6 to 6
- tile_count: int32 [8, 64], P('col', 'tile'), may hold values from 1 to 2, as said below
- tile_rows: int32 [8, 64, 2], P('col', 'tile'), may hold values from 1 to 255, as said below
Outputs:
- panel_adjoint: bfloat16 [8, 64, 2, 512, 512], P('col', 'tile')
- diag_adjoint: float32 [8, 512, 512], P('col', 'tile')
Inputs may be any that keep to these rules, and one draw needn't show every extreme that they name: `tile_count`: every device holds 1 to 2 live tiles of each panel column, in its first slots; in every column some device holds 2. `tile_rows`: in column c the live slots name distinct block rows; exactly one live slot names row c + 1, every other slot names a row of c + 2 or more. `diag_factor`: lower triangular with diagonal entries between 0.8 and 1.6. `diag_inverse`: lower triangular with diagonal entries between 0.8 and 1.6.
All inputs are finite; a program needn't handle non-finite values.
Results may differ from a plain program's by a relative error of at most 0.0044.
Values sent between devices are 32-bit elements; how exact they have to be, the bound alone decides.
No kernel may reach another device: no remote copies, remote signals or barrier semaphores. Data moves between devices by JAX's collectives and lax.ppermute only.
A program may use at most 128 MiB of HBM per device.

v0:
```python
import jax
import jax.numpy as jnp
from jax import lax
from jax.sharding import Mesh
from jax.sharding import PartitionSpec as P

TILE = ("y", "x", "core")
CHIPS = ("y", "x")


def swap_cores(value):
    return lax.ppermute(value, "core", [(0, 1), (1, 0)])


def all_sum(value):
    core = lax.axis_index("core")
    half = value.shape[0] // 2
    keep = lax.dynamic_slice_in_dim(value, core * half, half, 0)
    send = lax.dynamic_slice_in_dim(value, (1 - core) * half, half, 0)
    mine = keep + swap_cores(send)
    count = lax.axis_size(CHIPS)
    pieces = mine.reshape((count, half // count) + mine.shape[1:])
    share = jnp.sum(lax.all_to_all(pieces, CHIPS, 0, 0), axis=0)
    spread = jnp.broadcast_to(share[None], pieces.shape)
    mine = lax.all_to_all(spread, CHIPS, 0, 0).reshape(mine.shape)
    other = swap_cores(mine)
    whole = jnp.zeros(value.shape, value.dtype)
    whole = lax.dynamic_update_slice_in_dim(whole, mine, core * half, 0)
    return lax.dynamic_update_slice_in_dim(whole, other, (1 - core) * half, 0)


def symmetrize(matrix):
    rows = lax.broadcasted_iota(jnp.int32, matrix.shape, 0)
    cols = lax.broadcasted_iota(jnp.int32, matrix.shape, 1)
    return jnp.where(rows >= cols, matrix, matrix.T)


def on_device(
    panel_factor, panel_cotangent, diag_factor, diag_inverse, diag_cotangent, tile_count, tile_rows
):
    full = lax.Precision.HIGHEST
    chain = lax.Precision.HIGH
    factors = panel_factor[0, 0]
    cotangent = panel_cotangent[0, 0]
    lower = diag_factor[0]
    inverse = diag_inverse[0]
    width = lower.shape[0]
    rows_dev = diag_cotangent.shape[1]
    slot_count = factors.shape[0]
    column = lax.axis_index("col")
    groups = lax.axis_size("col")
    tile = lax.axis_index(TILE)
    core = lax.axis_index("core")
    row_start = tile * rows_dev
    live_slot = jnp.arange(slot_count) < tile_count[0, 0]
    link_flag = live_slot & (tile_rows[0, 0] == column + 1)
    solved = jnp.einsum("sij,jk->sik", cotangent, inverse, preferred_element_type=jnp.float32)
    rounded = jnp.where(
        live_slot[:, None, None], solved.astype(jnp.bfloat16), jnp.zeros_like(cotangent)
    )
    panel_terms = -jnp.einsum("sij,sik->jk", rounded, factors, preferred_element_type=jnp.float32)
    own_rows = lax.dynamic_slice_in_dim(panel_terms, row_start, rows_dev, 0) + diag_cotangent[0]
    panel_terms = lax.dynamic_update_slice_in_dim(panel_terms, own_rows, row_start, 0)
    chosen = jnp.sum(jnp.where(link_flag[:, None, None], factors, jnp.zeros_like(factors)), axis=0)
    link_part = jnp.dot(chosen, inverse, preferred_element_type=jnp.float32)
    reduced = all_sum(jnp.concatenate([panel_terms, link_part], axis=0))
    summed = reduced[:width]
    link_wide = reduced[width:]
    inverse_wide = inverse.astype(jnp.float32)
    curvature = jnp.dot(lower.astype(jnp.float32).T, summed, precision=full)
    symmetric = symmetrize(curvature)
    own_map = 0.5 * jnp.dot(
        inverse_wide.T, jnp.dot(symmetric, inverse_wide, precision=full), precision=full
    )
    half = width // 2
    down = [(i, i - 1) for i in range(1, groups)]

    def sweep(_, incoming):
        advanced = own_map + jnp.dot(
            link_wide.T, jnp.dot(incoming, link_wide, precision=chain), precision=chain
        )
        mine = lax.dynamic_slice_in_dim(advanced, core * half, half, 0)
        arrived = lax.ppermute(mine, "col", down)
        other = swap_cores(arrived)
        whole = jnp.zeros((width, width), jnp.float32)
        whole = lax.dynamic_update_slice_in_dim(whole, arrived, core * half, 0)
        return lax.dynamic_update_slice_in_dim(whole, other, (1 - core) * half, 0)

    incoming = lax.fori_loop(0, groups - 1, sweep, jnp.zeros((width, width), jnp.float32))
    product = jnp.dot(incoming, link_wide, precision=chain)
    link_rows = lax.dynamic_slice_in_dim(link_wide, row_start, rows_dev, 1)
    own_part = lax.dynamic_slice_in_dim(own_map, row_start, rows_dev, 0)
    diag_rows = own_part + jnp.dot(link_rows.T, product, precision=chain)
    adjusted = (solved - 2.0 * product[None]).astype(jnp.bfloat16)
    panel_out = jnp.where(link_flag[:, None, None], adjusted, rounded)
    return (panel_out[None, None], diag_rows[None])


def solution(mesh):
    cols, tiles = mesh.devices.shape
    split = Mesh(mesh.devices.reshape(cols, tiles // 8, 4, 2), ("col",) + TILE)
    in_specs = (
        P("col", TILE, None, None, None),
        P("col", TILE, None, None, None),
        P("col", None, None),
        P("col", None, None),
        P("col", TILE, None),
        P("col", TILE),
        P("col", TILE, None),
    )
    out_specs = (P("col", TILE, None, None, None), P("col", TILE, None))
    return jax.shard_map(
        on_device, mesh=split, in_specs=in_specs, out_specs=out_specs, check_vma=False
    )
```

profile of v0, /device:TPU:1, one launch (start us, length us, event | category | flops | bytes accessed | tf_op | source)
XLA Modules:
  0.0 307.1 jit_solution(11429396852032663570)
XLA Ops:
  1.9 3.1 %fusion.12 = f32[2,512,512]{2,1,0:T(8,128)} fusion(bf16[1,1,2,512,512]{4,3,2,1,0:T(8,128)(2,1)S(1)} %copy-done, bf16[1,512,512]{2,1,0:T(8,128)(2,1)} %param.12), kind=kOutput, calls=%fused_computation.27 | convolution fusion | flops 536870912 | bytes 3670016 | tf_op jit(solution)/shard_map/sij,jk->sik/dot_general | solution.py:57
  5.9 2.7 fusion
  10.0 8.7 %collective-permute-start.2 = (f32[512,512]{1,0:T(8,128)}, f32[512,512]{1,0:T(8,128)}, u32[]{:S(2)}, u32[]{:S(2)}) collective-permute-start(f32[512,512]{1,0:T(8,128)} %fusion.4), channel_id=1, source_target_pairs={{0,1},{1,0},{2,3},{3,2},{4,5},{5,4},{6,7},{7,6},{8,9},{9,8},{10,11... | collective-permute-start | bytes 3145736 | tf_op jit(solution)/shard_map/ppermute | solution.py:12
  18.7 2.6 collective-permute-done.2
  23.0 30.5 %all_to_all.10 = f32[32,16,512]{2,1,0:T(8,128)S(1)} all-to-all(f32[32,16,512]{2,1,0:T(8,128)S(1)} %bitcast.68), channel_id=1, replica_groups=mesh['col'=8,'y'=8,'x'=4,'core'=2] {'y','x'}, dimensions={0} | all-to-all | bytes 2097152 | tf_op jit(solution)/shard_map/all_to_all | solution.py:23
  53.7 31.7 %all_to_all.11 = f32[32,16,512]{2,1,0:T(8,128)S(1)} all-to-all(f32[32,16,512]{2,1,0:T(8,128)S(1)} %broadcast_in_dim.38), channel_id=1, replica_groups=mesh['col'=8,'y'=8,'x'=4,'core'=2] {'y','x'}, dimensions={0} | all-to-all | bytes 2097152 | tf_op jit(solution)/shard_map/all_to_all | solution.py:25
  85.3 5.5 %collective-permute-start.3 = (f32[512,512]{1,0:T(8,128)S(1)}, f32[512,512]{1,0:T(8,128)S(1)}, u32[]{:S(2)}, u32[]{:S(2)}) collective-permute-start(f32[512,512]{1,0:T(8,128)S(1)} %bitcast.69), channel_id=1, source_target_pairs={{0,1},{1,0},{2,3},{3,2},{4,5},{5,4},{6,7},{7,6},{8,9},{9,8},{10,11... | collective-permute-start | bytes 3145736 | tf_op jit(solution)/shard_map/ppermute | solution.py:12
  96.7 2.4 fusion.9
  99.1 2.1 convolution_multiply_fusion
  101.3 200.0 %while.12 = (s32[]{:T(128)}, f32[512,512]{0,1:T(8,128)S(1)}, f32[512,512]{1,0:T(8,128)S(1)}, f32[512,512]{1,0:T(8,128)}, s32[]{:T(128)}, /*index=5*/s32[]{:T(128)}, s32[]{:T(128)}, f32[]{:T(128)}) while((s32[]{:T(128)}, f32[512,512]{0,1:T(8,128)S(1)}, f32[512,512]{1,0:T(8,128)S(1)}, f32[512,512]{1,0:T(8,128)}, s32[]{:T(128)}, ...), condition=%wide.region_3.4_spmd, body=%wide.region_2.3_spmd.sunk | while | flops 1610743808 | bytes 21496020 | solution.py:89
  104.4 2.0 copy.15
  108.9 14.7 %collective-permute-done = f32[256,512]{0,1:T(8,128)} collective-permute-done((f32[256,512]{0,1:T(8,128)S(1)}, f32[256,512]{0,1:T(8,128)}, u32[]{:S(2)}, u32[]{:S(2)}) %collective-permute-start) | collective-permute-done | bytes 524320 | tf_op jit(solution)/shard_map/while/body/eval_jaxpr/ppermute | solution.py:83
  123.6 2.8 collective-permute-start.1
  132.5 2.0 copy.15
  137.0 14.8 %collective-permute-done = f32[256,512]{0,1:T(8,128)} collective-permute-done((f32[256,512]{0,1:T(8,128)S(1)}, f32[256,512]{0,1:T(8,128)}, u32[]{:S(2)}, u32[]{:S(2)}) %collective-permute-start) | collective-permute-done | bytes 524320 | tf_op jit(solution)/shard_map/while/body/eval_jaxpr/ppermute | solution.py:83
  151.8 2.8 collective-permute-start.1
  160.7 2.0 copy.15
  165.2 14.7 %collective-permute-done = f32[256,512]{0,1:T(8,128)} collective-permute-done((f32[256,512]{0,1:T(8,128)S(1)}, f32[256,512]{0,1:T(8,128)}, u32[]{:S(2)}, u32[]{:S(2)}) %collective-permute-start) | collective-permute-done | bytes 524320 | tf_op jit(solution)/shard_map/while/body/eval_jaxpr/ppermute | solution.py:83
  180.0 2.8 collective-permute-start.1
  188.9 2.0 copy.15
  193.4 16.0 %collective-permute-done = f32[256,512]{0,1:T(8,128)} collective-permute-done((f32[256,512]{0,1:T(8,128)S(1)}, f32[256,512]{0,1:T(8,128)}, u32[]{:S(2)}, u32[]{:S(2)}) %collective-permute-start) | collective-permute-done | bytes 524320 | tf_op jit(solution)/shard_map/while/body/eval_jaxpr/ppermute | solution.py:83
  209.3 2.8 collective-permute-start.1
  218.2 2.0 copy.15
  222.7 15.3 %collective-permute-done = f32[256,512]{0,1:T(8,128)} collective-permute-done((f32[256,512]{0,1:T(8,128)S(1)}, f32[256,512]{0,1:T(8,128)}, u32[]{:S(2)}, u32[]{:S(2)}) %collective-permute-start) | collective-permute-done | bytes 524320 | tf_op jit(solution)/shard_map/while/body/eval_jaxpr/ppermute | solution.py:83
  238.0 2.8 collective-permute-start.1
  246.9 2.0 copy.15
  251.4 15.3 %collective-permute-done = f32[256,512]{0,1:T(8,128)} collective-permute-done((f32[256,512]{0,1:T(8,128)S(1)}, f32[256,512]{0,1:T(8,128)}, u32[]{:S(2)}, u32[]{:S(2)}) %collective-permute-start) | collective-permute-done | bytes 524320 | tf_op jit(solution)/shard_map/while/body/eval_jaxpr/ppermute | solution.py:83
  266.8 2.8 collective-permute-start.1
  275.7 2.0 copy.15
  280.2 15.3 %collective-permute-done = f32[256,512]{0,1:T(8,128)} collective-permute-done((f32[256,512]{0,1:T(8,128)S(1)}, f32[256,512]{0,1:T(8,128)}, u32[]{:S(2)}, u32[]{:S(2)}) %collective-permute-start) | collective-permute-done | bytes 524320 | tf_op jit(solution)/shard_map/while/body/eval_jaxpr/ppermute | solution.py:83
  295.5 2.8 collective-permute-start.1
  301.3 2.4 broadcast_multiply_fusion
  (113 shorter events, 73.0 us)
Async XLA Ops:
  0.6 1.2 copy-start
  0.6 4.4 %copy-start.9 = (s32[1,1,2]{2,1,0:T(1,128)S(1)}, s32[1,1,2]{2,1,0:T(1,128)}, u32[]{:S(2)}) copy-start(s32[1,1,2]{2,1,0:T(1,128)} %param.15) | copy-start | bytes 28
  0.7 4.4 %copy-start.6 = (bf16[1,1,2,512,512]{4,3,2,1,0:T(8,128)(2,1)S(1)}, bf16[1,1,2,512,512]{4,3,2,1,0:T(8,128)(2,1)}, u32[]{:S(2)}) copy-start(bf16[1,1,2,512,512]{4,3,2,1,0:T(8,128)(2,1)} %param.9) | copy-start | bytes 3145732
  1.9 3.6 %copy-start.4 = (bf16[1,512,512]{2,1,0:T(8,128)(2,1)S(1)}, bf16[1,512,512]{2,1,0:T(8,128)(2,1)}, u32[]{:S(2)}) copy-start(bf16[1,512,512]{2,1,0:T(8,128)(2,1)} %param.12) | copy-start | bytes 1572868
  5.9 2.7 copy-start.8
  10.0 11.4 %collective-permute-start.2 = (f32[512,512]{1,0:T(8,128)}, f32[512,512]{1,0:T(8,128)}, u32[]{:S(2)}, u32[]{:S(2)}) collective-permute-start(f32[512,512]{1,0:T(8,128)} %fusion.4), channel_id=1, source_target_pairs={{0,1},{1,0},{2,3},{3,2},{4,5},{5,4},{6,7},{7,6},{8,9},{9,8},{10,11... | collective-permute-start | bytes 3145736 | tf_op jit(solution)/shard_map/ppermute | solution.py:12
  85.3 7.6 %collective-permute-start.3 = (f32[512,512]{1,0:T(8,128)S(1)}, f32[512,512]{1,0:T(8,128)S(1)}, u32[]{:S(2)}, u32[]{:S(2)}) collective-permute-start(f32[512,512]{1,0:T(8,128)S(1)} %bitcast.69), channel_id=1, source_target_pairs={{0,1},{1,0},{2,3},{3,2},{4,5},{5,4},{6,7},{7,6},{8,9},{9,8},{10,11... | collective-permute-start | bytes 3145736 | tf_op jit(solution)/shard_map/ppermute | solution.py:12
  91.2 3.1 %copy-start.7 = (bf16[1,512,512]{2,1,0:T(8,128)(2,1)S(1)}, bf16[1,512,512]{2,1,0:T(8,128)(2,1)}, u32[]{:S(2)}) copy-start(bf16[1,512,512]{2,1,0:T(8,128)(2,1)} %param.11) | copy-start | bytes 1572868
  93.0 1.3 copy-start.1
  96.7 2.4 copy-start.5
  102.3 1.2 copy-start.2
  107.6 16.0 %collective-permute-start = (f32[256,512]{0,1:T(8,128)S(1)}, f32[256,512]{0,1:T(8,128)}, u32[]{:S(2)}, u32[]{:S(2)}) collective-permute-start(f32[256,512]{0,1:T(8,128)S(1)} %dynamic-slice_add_fusion.2), channel_id=1, source_target_pairs={{64,0},{128,64},{192,128},{256,192},{320,256},{384,320},{448,384},... | collective-permute-start | bytes 1572872 | tf_op jit(solution)/shard_map/while/body/eval_jaxpr/ppermute | solution.py:83
  123.6 4.7 %collective-permute-start.1 = (f32[256,512]{0,1:T(8,128)}, f32[256,512]{0,1:T(8,128)}, u32[]{:S(2)}, u32[]{:S(2)}) collective-permute-start(f32[256,512]{0,1:T(8,128)} %collective-permute-done), channel_id=1, source_target_pairs={{0,1},{1,0},{2,3},{3,2},{4,5},{5,4},{6,7},{7,6},{8,9},{9,8},{10,11... | collective-permute-start | bytes 1572872 | tf_op jit(solution)/shard_map/while/body/eval_jaxpr/ppermute | solution.py:12
  130.5 1.2 copy-start.2
  135.7 16.1 %collective-permute-start = (f32[256,512]{0,1:T(8,128)S(1)}, f32[256,512]{0,1:T(8,128)}, u32[]{:S(2)}, u32[]{:S(2)}) collective-permute-start(f32[256,512]{0,1:T(8,128)S(1)} %dynamic-slice_add_fusion.2), channel_id=1, source_target_pairs={{64,0},{128,64},{192,128},{256,192},{320,256},{384,320},{448,384},... | collective-permute-start | bytes 1572872 | tf_op jit(solution)/shard_map/while/body/eval_jaxpr/ppermute | solution.py:83
  151.8 4.7 %collective-permute-start.1 = (f32[256,512]{0,1:T(8,128)}, f32[256,512]{0,1:T(8,128)}, u32[]{:S(2)}, u32[]{:S(2)}) collective-permute-start(f32[256,512]{0,1:T(8,128)} %collective-permute-done), channel_id=1, source_target_pairs={{0,1},{1,0},{2,3},{3,2},{4,5},{5,4},{6,7},{7,6},{8,9},{9,8},{10,11... | collective-permute-start | bytes 1572872 | tf_op jit(solution)/shard_map/while/body/eval_jaxpr/ppermute | solution.py:12
  158.7 1.2 copy-start.2
  163.9 16.0 %collective-permute-start = (f32[256,512]{0,1:T(8,128)S(1)}, f32[256,512]{0,1:T(8,128)}, u32[]{:S(2)}, u32[]{:S(2)}) collective-permute-start(f32[256,512]{0,1:T(8,128)S(1)} %dynamic-slice_add_fusion.2), channel_id=1, source_target_pairs={{64,0},{128,64},{192,128},{256,192},{320,256},{384,320},{448,384},... | collective-permute-start | bytes 1572872 | tf_op jit(solution)/shard_map/while/body/eval_jaxpr/ppermute | solution.py:83
  180.0 4.7 %collective-permute-start.1 = (f32[256,512]{0,1:T(8,128)}, f32[256,512]{0,1:T(8,128)}, u32[]{:S(2)}, u32[]{:S(2)}) collective-permute-start(f32[256,512]{0,1:T(8,128)} %collective-permute-done), channel_id=1, source_target_pairs={{0,1},{1,0},{2,3},{3,2},{4,5},{5,4},{6,7},{7,6},{8,9},{9,8},{10,11... | collective-permute-start | bytes 1572872 | tf_op jit(solution)/shard_map/while/body/eval_jaxpr/ppermute | solution.py:12
  186.8 1.2 copy-start.2
  192.1 17.3 %collective-permute-start = (f32[256,512]{0,1:T(8,128)S(1)}, f32[256,512]{0,1:T(8,128)}, u32[]{:S(2)}, u32[]{:S(2)}) collective-permute-start(f32[256,512]{0,1:T(8,128)S(1)} %dynamic-slice_add_fusion.2), channel_id=1, source_target_pairs={{64,0},{128,64},{192,128},{256,192},{320,256},{384,320},{448,384},... | collective-permute-start | bytes 1572872 | tf_op jit(solution)/shard_map/while/body/eval_jaxpr/ppermute | solution.py:83
  209.3 4.7 %collective-permute-start.1 = (f32[256,512]{0,1:T(8,128)}, f32[256,512]{0,1:T(8,128)}, u32[]{:S(2)}, u32[]{:S(2)}) collective-permute-start(f32[256,512]{0,1:T(8,128)} %collective-permute-done), channel_id=1, source_target_pairs={{0,1},{1,0},{2,3},{3,2},{4,5},{5,4},{6,7},{7,6},{8,9},{9,8},{10,11... | collective-permute-start | bytes 1572872 | tf_op jit(solution)/shard_map/while/body/eval_jaxpr/ppermute | solution.py:12
  216.2 1.2 copy-start.2
  221.4 16.6 %collective-permute-start = (f32[256,512]{0,1:T(8,128)S(1)}, f32[256,512]{0,1:T(8,128)}, u32[]{:S(2)}, u32[]{:S(2)}) collective-permute-start(f32[256,512]{0,1:T(8,128)S(1)} %dynamic-slice_add_fusion.2), channel_id=1, source_target_pairs={{64,0},{128,64},{192,128},{256,192},{320,256},{384,320},{448,384},... | collective-permute-start | bytes 1572872 | tf_op jit(solution)/shard_map/while/body/eval_jaxpr/ppermute | solution.py:83
  238.0 4.7 %collective-permute-start.1 = (f32[256,512]{0,1:T(8,128)}, f32[256,512]{0,1:T(8,128)}, u32[]{:S(2)}, u32[]{:S(2)}) collective-permute-start(f32[256,512]{0,1:T(8,128)} %collective-permute-done), channel_id=1, source_target_pairs={{0,1},{1,0},{2,3},{3,2},{4,5},{5,4},{6,7},{7,6},{8,9},{9,8},{10,11... | collective-permute-start | bytes 1572872 | tf_op jit(solution)/shard_map/while/body/eval_jaxpr/ppermute | solution.py:12
  244.9 1.2 copy-start.2
  250.1 16.6 %collective-permute-start = (f32[256,512]{0,1:T(8,128)S(1)}, f32[256,512]{0,1:T(8,128)}, u32[]{:S(2)}, u32[]{:S(2)}) collective-permute-start(f32[256,512]{0,1:T(8,128)S(1)} %dynamic-slice_add_fusion.2), channel_id=1, source_target_pairs={{64,0},{128,64},{192,128},{256,192},{320,256},{384,320},{448,384},... | collective-permute-start | bytes 1572872 | tf_op jit(solution)/shard_map/while/body/eval_jaxpr/ppermute | solution.py:83
  266.8 4.7 %collective-permute-start.1 = (f32[256,512]{0,1:T(8,128)}, f32[256,512]{0,1:T(8,128)}, u32[]{:S(2)}, u32[]{:S(2)}) collective-permute-start(f32[256,512]{0,1:T(8,128)} %collective-permute-done), channel_id=1, source_target_pairs={{0,1},{1,0},{2,3},{3,2},{4,5},{5,4},{6,7},{7,6},{8,9},{9,8},{10,11... | collective-permute-start | bytes 1572872 | tf_op jit(solution)/shard_map/while/body/eval_jaxpr/ppermute | solution.py:12
  273.6 1.2 copy-start.2
  278.9 16.6 %collective-permute-start = (f32[256,512]{0,1:T(8,128)S(1)}, f32[256,512]{0,1:T(8,128)}, u32[]{:S(2)}, u32[]{:S(2)}) collective-permute-start(f32[256,512]{0,1:T(8,128)S(1)} %dynamic-slice_add_fusion.2), channel_id=1, source_target_pairs={{64,0},{128,64},{192,128},{256,192},{320,256},{384,320},{448,384},... | collective-permute-start | bytes 1572872 | tf_op jit(solution)/shard_map/while/body/eval_jaxpr/ppermute | solution.py:83
  295.5 4.7 %collective-permute-start.1 = (f32[256,512]{0,1:T(8,128)}, f32[256,512]{0,1:T(8,128)}, u32[]{:S(2)}, u32[]{:S(2)}) collective-permute-start(f32[256,512]{0,1:T(8,128)} %collective-permute-done), channel_id=1, source_target_pairs={{0,1},{1,0},{2,3},{3,2},{4,5},{5,4},{6,7},{7,6},{8,9},{9,8},{10,11... | collective-permute-start | bytes 1572872 | tf_op jit(solution)/shard_map/while/body/eval_jaxpr/ppermute | solution.py:12
  301.3 4.2 %copy-start.3 = (f32[2,512,512]{2,1,0:T(8,128)S(1)}, f32[2,512,512]{2,1,0:T(8,128)}, u32[]{:S(2)}) copy-start(f32[2,512,512]{2,1,0:T(8,128)} %fusion.12) | copy-start | bytes 6291460
where the time goes:
time: 311 us; the launch traced here: 307 us
  waiting for transfers between devices  115 us (37%)
  blocking collectives  62.1 us (20%)
  starting transfers between devices  43.1 us (14%)
  local copies, waits for them, and re-layouts  41.4 us (13%)
  matrix products  30.3 us (10%)
  other arithmetic  13.2 us (4%)
    ppermute x7, waiting for transfers between devices, sweep(): arrived = lax.ppermute(mine, 'col', down)  106 us
    ppermute x9, starting transfers between devices, swap_cores(): return lax.ppermute(value, 'core', [(0, 1), (1, 0)])  34 us
    all_to_all x1, blocking collectives, all_sum(): mine = lax.all_to_all(spread, CHIPS, 0, 0).reshape(mine.shape)  31.7 us
    all_to_all x1, blocking collectives, all_sum(): share = jnp.sum(lax.all_to_all(pieces, CHIPS, 0, 0), axis=0)  30.5 us
    dynamic_slice x14, local copies, waits for them, and re-layouts, sweep(): mine = lax.dynamic_slice_in_dim(advanced, core * half, half, 0)  20.1 us
    ppermute x7, starting transfers between devices, sweep(): arrived = lax.ppermute(mine, 'col', down)  9.04 us
    ppermute x9, waiting for transfers between devices, swap_cores(): return lax.ppermute(value, 'core', [(0, 1), (1, 0)])  8.64 us
    add x7, other arithmetic, sweep(): own_map + jnp.dot(link_wide.T, jnp.dot(incoming, link_wide, precision=cha...  8.09 us
  transfers between devices with their start and end apart: 16, of which 16 were waited for; matrix products, arithmetic and copies ran while one was open for 3% of the time, Pallas kernels for 0%

commit v1 on v0

--- a/solution.py
+++ b/solution.py
@@ -27,6 +27,38 @@
     whole = jnp.zeros(value.shape, value.dtype)
     whole = lax.dynamic_update_slice_in_dim(whole, mine, core * half, 0)
     return lax.dynamic_update_slice_in_dim(whole, other, (1 - core) * half, 0)
+
+
+BLOCKS = 4
+
+
+def pack(matrix):
+    size = matrix.shape[0] // BLOCKS
+    return jnp.concatenate(
+        [
+            matrix[i * size : (i + 1) * size, j * size : (j + 1) * size]
+            for i in range(BLOCKS)
+            for j in range(i + 1)
+        ],
+        axis=0,
+    )
+
+
+def unpack(packed, width):
+    size = width // BLOCKS
+    blocks = {}
+    k = 0
+    for i in range(BLOCKS):
+        for j in range(i + 1):
+            blocks[i, j] = packed[k * size : (k + 1) * size]
+            k += 1
+    rows = [
+        jnp.concatenate(
+            [blocks[i, j] if i >= j else blocks[j, i].T for j in range(BLOCKS)], axis=1
+        )
+        for i in range(BLOCKS)
+    ]
+    return jnp.concatenate(rows, axis=0)
 
 
 def symmetrize(matrix):
@@ -72,21 +104,19 @@
     own_map = 0.5 * jnp.dot(
         inverse_wide.T, jnp.dot(symmetric, inverse_wide, precision=full), precision=full
     )
-    half = width // 2
-    down = [(i, i - 1) for i in range(1, groups)]
+    down = [(2 * i, 2 * (i - 1)) for i in range(1, groups)]
 
-    def sweep(_, incoming):
+    def sweep(_, packed):
+        incoming = unpack(packed, width)
         advanced = own_map + jnp.dot(
             link_wide.T, jnp.dot(incoming, link_wide, precision=chain), precision=chain
         )
-        mine = lax.dynamic_slice_in_dim(advanced, core * half, half, 0)
-        arrived = lax.ppermute(mine, "col", down)
-        other = swap_cores(arrived)
-        whole = jnp.zeros((width, width), jnp.float32)
-        whole = lax.dynamic_update_slice_in_dim(whole, arrived, core * half, 0)
-        return lax.dynamic_update_slice_in_dim(whole, other, (1 - core) * half, 0)
+        return lax.ppermute(pack(advanced), ("col", "core"), down)
 
-    incoming = lax.fori_loop(0, groups - 1, sweep, jnp.zeros((width, width), jnp.float32))
+    start = jnp.zeros((BLOCKS * (BLOCKS + 1) // 2 * width // BLOCKS, width // BLOCKS), jnp.float32)
+    packed = lax.fori_loop(0, groups - 1, sweep, start)
+    shared = lax.ppermute(packed, "core", [(0, 1)])
+    incoming = unpack(jnp.where(core == 0, packed, shared), width)
     product = jnp.dot(incoming, link_wide, precision=chain)
     link_rows = lax.dynamic_slice_in_dim(link_wide, row_start, rows_dev, 1)
     own_part = lax.dynamic_slice_in_dim(own_map, row_start, rows_dev, 0)

time: 311 us -> 248 us (0.80)
  starting transfers between devices: 43.1 us -> 20.5 us
  local copies, waits for them, and re-layouts: 41.4 us -> 20.2 us
  waiting for transfers between devices: 115 us -> 94.9 us
  matrix products: 30.3 us -> 38.1 us
  other arithmetic: 13.2 us -> 7.13 us
    dynamic_slice x14 -> x0, local copies, waits for them, and re-layouts: 20.1 us -> none  [sweep(): mine = lax.dynamic_slice_in_dim(advanced, core * half, half, 0)]
    ppermute x9 -> x2, starting transfers between devices: 34 us -> 14.3 us  [swap_cores(): return lax.ppermute(value, 'core', [(0, 1), (1, 0)])]
    ppermute x7 -> x8, waiting for transfers between devices: 106 us -> 90.4 us  [the longest x1 90.4 us: on_device(): shared = lax.ppermute(packed, 'core', [(0, 1)])]
    dynamic_update_slice x14 -> x0, local copies, waits for them, and re-layouts: 15.5 us -> none  [the longest x7 7.76 us: sweep(): whole = lax.dynamic_update_slice_in_dim(whole, arrived, core * half, 0)]
    add x7 -> x0, other arithmetic: 8.09 us -> none  [sweep(): own_map + jnp.dot(link_wide.T, jnp.dot(incoming, link_wide, precision=cha...]
    dot_general x7, matrix products: 7.17 us -> 14.9 us  [sweep(): jnp.dot(incoming, link_wide, precision=chain)]
    slice x0 -> x29, local copies, waits for them, and re-layouts: none -> 7.2 us  [unpack(): blocks[i, j] = packed[k * size:(k + 1) * size]]
    transpose x0 -> x7, local copies, waits for them, and re-layouts: none -> 4.93 us  [unpack(): blocks[j, i]]
  transfers between devices with their start and end apart: 16 -> 10, of which waited for: 16 -> 3; matrix products, arithmetic and copies ran while one was open for 3% -> 0% of each run, Pallas kernels for 0% -> 0%
where the time goes in v1:
time: 248 us; the launch traced here: 246 us
  waiting for transfers between devices  94.9 us (38%)
  blocking collectives  61.8 us (25%)
  matrix products  38.1 us (15%)
  starting transfers between devices  20.5 us (8%)
  local copies, waits for them, and re-layouts  20.2 us (8%)
  other arithmetic  7.13 us (3%)
    ppermute x1, waiting for transfers between devices, on_device(): shared = lax.ppermute(packed, 'core', [(0, 1)])  90.4 us
    all_to_all x1, blocking collectives, all_sum(): mine = lax.all_to_all(spread, CHIPS, 0, 0).reshape(mine.shape)  31.5 us
    all_to_all x1, blocking collectives, all_sum(): share = jnp.sum(lax.all_to_all(pieces, CHIPS, 0, 0), axis=0)  30.3 us
    dot_general x7, matrix products, sweep(): jnp.dot(incoming, link_wide, precision=chain)  14.9 us
    ppermute x2, starting transfers between devices, swap_cores(): return lax.ppermute(value, 'core', [(0, 1), (1, 0)])  14.3 us
    dot_general x7, matrix products, sweep(): jnp.dot(link_wide.T, jnp.dot(incoming, link_wide, precision=chain), preci...  7.33 us
    slice x29, local copies, waits for them, and re-layouts, unpack(): blocks[i, j] = packed[k * size:(k + 1) * size]  7.2 us
  transfers between devices with their start and end apart: 10, of which 3 were waited for; matrix products, arithmetic and copies ran while one was open for 0% of the time, Pallas kernels for 0%

profile of v1, /device:TPU:1, one launch (start us, length us, event | category | flops | bytes accessed | tf_op | source)
XLA Modules:
  0.0 245.6 jit_solution(17591207055564976655)
XLA Ops:
  2.1 1.6 fusion.65
  3.7 1.5 fusion.72
  5.2 2.0 fusion.66
  7.2 2.7 %fusion.28 = f32[512,512]{1,0:T(8,128)S(1)} fusion(bf16[1,1,2,512,512]{4,3,2,1,0:T(8,128)(2,1)} %param.9, f32[2,512,512]{2,1,0:T(8,128)} %fusion.66, pred[2]{0:T(512)(128)(4,1)S(1)} %get-tuple-element.64), kind=kOutput, calls=%fused_computation.52 | convolution fusion | flops 538181632 | bytes 4194306 | tf_op jit(solution)/shard_map/sij,sik->jk/dot_general | solution.py:93
  10.9 1.4 fusion.32
  12.3 8.7 %collective-permute-start.1 = (f32[512,512]{1,0:T(8,128)}, f32[512,512]{1,0:T(8,128)}, u32[]{:S(2)}, u32[]{:S(2)}) collective-permute-start(f32[512,512]{1,0:T(8,128)} %fusion.32), channel_id=1, source_target_pairs={{0,1},{1,0},{2,3},{3,2},{4,5},{5,4},{6,7},{7,6},{8,9},{9,8},{10,11... | collective-permute-start | bytes 3145736 | tf_op jit(solution)/shard_map/ppermute | solution.py:12
  21.1 2.6 %collective-permute-done.1 = f32[512,512]{1,0:T(8,128)} collective-permute-done((f32[512,512]{1,0:T(8,128)}, f32[512,512]{1,0:T(8,128)}, u32[]{:S(2)}, u32[]{:S(2)}) %collective-permute-start.1) | collective-permute-done | bytes 1048608 | tf_op jit(solution)/shard_map/ppermute | solution.py:12
  23.7 1.6 fusion.34
  25.3 30.3 %all_to_all.10 = f32[32,16,512]{2,1,0:T(8,128)S(1)} all-to-all(f32[32,16,512]{2,1,0:T(8,128)S(1)} %bitcast.88), channel_id=1, replica_groups=mesh['col'=8,'y'=8,'x'=4,'core'=2] {'y','x'}, dimensions={0} | all-to-all | bytes 2097152 | tf_op jit(solution)/shard_map/all_to_all | solution.py:23
  55.8 31.5 %all_to_all.11 = f32[32,16,512]{2,1,0:T(8,128)S(1)} all-to-all(f32[32,16,512]{2,1,0:T(8,128)S(1)} %broadcast_in_dim.42), channel_id=1, replica_groups=mesh['col'=8,'y'=8,'x'=4,'core'=2] {'y','x'}, dimensions={0} | all-to-all | bytes 2097152 | tf_op jit(solution)/shard_map/all_to_all | solution.py:25
  87.3 5.6 %collective-permute-start.2 = (f32[512,512]{1,0:T(8,128)S(1)}, f32[512,512]{1,0:T(8,128)S(1)}, u32[]{:S(2)}, u32[]{:S(2)}) collective-permute-start(f32[512,512]{1,0:T(8,128)S(1)} %bitcast.89), channel_id=1, source_target_pairs={{0,1},{1,0},{2,3},{3,2},{4,5},{5,4},{6,7},{7,6},{8,9},{9,8},{10,11... | collective-permute-start | bytes 3145736 | tf_op jit(solution)/shard_map/ppermute | solution.py:12
  93.2 1.9 collective-permute-done.2
  95.3 1.2 copy-done.5
  97.5 1.3 copy.19
  98.8 2.4 fusion.63
  101.3 2.1 convolution_multiply_fusion
  103.4 43.9 %while.10 = (s32[]{:T(128)}, f32[1280,128]{1,0:T(8,128)S(1)}, f32[512,512]{1,0:T(8,128)S(1)}, f32[512,512]{1,0:T(8,128)}, s32[]{:T(128)}) while((s32[]{:T(128)}, f32[1280,128]{1,0:T(8,128)S(1)}, f32[512,512]{1,0:T(8,128)S(1)}, f32[512,512]{1,0:T(8,128)}, s32[]{:T(128)}) %tuple.56), condition=%wide.region_3.4_spmd, body=%wide.region_2.3_spmd.sunk | while | flops 1614217216 | bytes 19923072 | solution.py:117
  105.5 2.1 fusion.102
  107.7 1.1 fusion.103
  111.8 2.1 fusion.102
  118.1 2.1 fusion.102
  120.2 1.0 fusion.103
  124.4 2.1 fusion.102
  130.6 2.1 fusion.102
  132.8 1.0 fusion.103
  136.9 2.1 fusion.102
  143.2 2.1 fusion.102
  147.3 1.3 collective-permute-start.3
  148.6 90.4 %collective-permute-done.3 = f32[1280,128]{1,0:T(8,128)S(1)} collective-permute-done((f32[1280,128]{1,0:T(8,128)S(1)}, f32[1280,128]{1,0:T(8,128)S(1)}, u32[]{:S(2)}, u32[]{:S(2)}) %collective-permute-start.3) | collective-permute-done | bytes 655392 | tf_op jit(solution)/shard_map/ppermute | solution.py:118
  239.8 2.4 broadcast_multiply_fusion
  242.2 1.9 fusion.29
  244.0 1.6 fusion.31
  (185 shorter events, 28.8 us)
Async XLA Ops:
  0.6 4.5 %copy-start = (bf16[1,1,2,512,512]{4,3,2,1,0:T(8,128)(2,1)S(1)}, bf16[1,1,2,512,512]{4,3,2,1,0:T(8,128)(2,1)}, u32[]{:S(2)}) copy-start(bf16[1,1,2,512,512]{4,3,2,1,0:T(8,128)(2,1)} %param.10) | copy-start | bytes 3145732
  0.6 4.5 %copy-start.3 = (bf16[1,512,512]{2,1,0:T(8,128)(2,1)S(1)}, bf16[1,512,512]{2,1,0:T(8,128)(2,1)}, u32[]{:S(2)}) copy-start(bf16[1,512,512]{2,1,0:T(8,128)(2,1)} %param.12) | copy-start | bytes 1572868
  7.2 2.7 %copy-start.8 = (f32[1,8,512]{2,1,0:T(8,128)S(1)}, f32[1,8,512]{2,1,0:T(8,128)}, u32[]{:S(2)}) copy-start(f32[1,8,512]{2,1,0:T(8,128)} %param.13) | copy-start | bytes 49156
  9.9 1.0 copy-start.6
  12.3 11.4 %collective-permute-start.1 = (f32[512,512]{1,0:T(8,128)}, f32[512,512]{1,0:T(8,128)}, u32[]{:S(2)}, u32[]{:S(2)}) collective-permute-start(f32[512,512]{1,0:T(8,128)} %fusion.32), channel_id=1, source_target_pairs={{0,1},{1,0},{2,3},{3,2},{4,5},{5,4},{6,7},{7,6},{8,9},{9,8},{10,11... | collective-permute-start | bytes 3145736 | tf_op jit(solution)/shard_map/ppermute | solution.py:12
  87.3 7.8 %collective-permute-start.2 = (f32[512,512]{1,0:T(8,128)S(1)}, f32[512,512]{1,0:T(8,128)S(1)}, u32[]{:S(2)}, u32[]{:S(2)}) collective-permute-start(f32[512,512]{1,0:T(8,128)S(1)} %bitcast.89), channel_id=1, source_target_pairs={{0,1},{1,0},{2,3},{3,2},{4,5},{5,4},{6,7},{7,6},{8,9},{9,8},{10,11... | collective-permute-start | bytes 3145736 | tf_op jit(solution)/shard_map/ppermute | solution.py:12
  93.2 3.3 %copy-start.7 = (bf16[1,512,512]{2,1,0:T(8,128)(2,1)S(1)}, bf16[1,512,512]{2,1,0:T(8,128)(2,1)}, u32[]{:S(2)}) copy-start(bf16[1,512,512]{2,1,0:T(8,128)(2,1)} %param.11) | copy-start | bytes 1572868
  95.2 1.3 copy-start.5
  98.8 2.4 copy-start.4
  105.5 2.2 copy-start.1
  108.9 0.7 collective-permute-start
  111.8 2.1 copy-start.1
  115.2 0.7 collective-permute-start
  118.1 2.1 copy-start.1
  121.5 0.7 collective-permute-start
  124.3 2.1 copy-start.1
  127.7 0.7 collective-permute-start
  130.6 2.1 copy-start.1
  134.0 0.7 collective-permute-start
  136.9 2.1 copy-start.1
  140.3 0.7 collective-permute-start
  143.2 2.1 copy-start.1
  146.6 0.7 collective-permute-start
  147.3 91.7 %collective-permute-start.3 = (f32[1280,128]{1,0:T(8,128)S(1)}, f32[1280,128]{1,0:T(8,128)S(1)}, u32[]{:S(2)}, u32[]{:S(2)}) collective-permute-start(f32[1280,128]{1,0:T(8,128)S(1)} %get-tuple-element.24), channel_id=1, source_target_pairs={{0,1},{2,3},{4,5},{6,7},{8,9},{10,11},{12,13},{14,15},{16,17},{18,... | collective-permute-start | bytes 1966088 | tf_op jit(solution)/shard_map/ppermute | solution.py:118
  239.8 4.2 %copy-start.2 = (f32[2,512,512]{2,1,0:T(8,128)S(1)}, f32[2,512,512]{2,1,0:T(8,128)}, u32[]{:S(2)}) copy-start(f32[2,512,512]{2,1,0:T(8,128)} %fusion.66) | copy-start | bytes 6291460

commit v2 on v1

--- a/solution.py
+++ b/solution.py
@@ -12,17 +12,29 @@
     return lax.ppermute(value, "core", [(0, 1), (1, 0)])
 
 
+def scatter_sum(value, axis):
+    count = lax.axis_size(axis)
+    pieces = value.reshape((count, value.shape[0] // count) + value.shape[1:])
+    return jnp.sum(lax.all_to_all(pieces, axis, 0, 0), axis=0)
+
+
+def gather_all(value, axis):
+    count = lax.axis_size(axis)
+    spread = jnp.broadcast_to(value[None], (count,) + value.shape)
+    gathered = lax.all_to_all(spread, axis, 0, 0)
+    return gathered.reshape((count * value.shape[0],) + value.shape[1:])
+
+
 def all_sum(value):
     core = lax.axis_index("core")
     half = value.shape[0] // 2
     keep = lax.dynamic_slice_in_dim(value, core * half, half, 0)
     send = lax.dynamic_slice_in_dim(value, (1 - core) * half, half, 0)
     mine = keep + swap_cores(send)
-    count = lax.axis_size(CHIPS)
-    pieces = mine.reshape((count, half // count) + mine.shape[1:])
-    share = jnp.sum(lax.all_to_all(pieces, CHIPS, 0, 0), axis=0)
-    spread = jnp.broadcast_to(share[None], pieces.shape)
-    mine = lax.all_to_all(spread, CHIPS, 0, 0).reshape(mine.shape)
+    for axis in CHIPS[::-1]:
+        mine = scatter_sum(mine, axis)
+    for axis in CHIPS:
+        mine = gather_all(mine, axis)
     other = swap_cores(mine)
     whole = jnp.zeros(value.shape, value.dtype)
     whole = lax.dynamic_update_slice_in_dim(whole, mine, core * half, 0)

time: 248 us -> 246 us (level)
  blocking collectives: 61.8 us -> 53.7 us
    all_to_all x2 -> x4, blocking collectives: 61.8 us -> 53.7 us  [the longest x2 28.6 us: scatter_sum(): return jnp.sum(lax.all_to_all(pieces, axis, 0, 0), axis=0)]
where the time goes in v2:
time: 246 us; the launch traced here: 243 us
  waiting for transfers between devices  95.1 us (39%)
  blocking collectives  53.7 us (22%)
  matrix products  39.2 us (16%)
  local copies, waits for them, and re-layouts  22.5 us (9%)
  starting transfers between devices  22.2 us (9%)
  other arithmetic  7.17 us (3%)
    ppermute x1, waiting for transfers between devices, on_device(): shared = lax.ppermute(packed, 'core', [(0, 1)])  90.4 us
    all_to_all x2, blocking collectives, scatter_sum(): return jnp.sum(lax.all_to_all(pieces, axis, 0, 0), axis=0)  28.6 us
    all_to_all x2, blocking collectives, gather_all(): gathered = lax.all_to_all(spread, axis, 0, 0)  25.1 us
    ppermute x2, starting transfers between devices, swap_cores(): return lax.ppermute(value, 'core', [(0, 1), (1, 0)])  16 us
    dot_general x7, matrix products, sweep(): jnp.dot(incoming, link_wide, precision=chain)  14.9 us
    dot_general x7, matrix products, sweep(): jnp.dot(link_wide.T, jnp.dot(incoming, link_wide, precision=chain), preci...  7.32 us
    slice x29, local copies, waits for them, and re-layouts, unpack(): blocks[i, j] = packed[k * size:(k + 1) * size]  7.09 us
    transpose x7, local copies, waits for them, and re-layouts, unpack(): blocks[j, i]  4.94 us
  transfers between devices with their start and end apart: 10, of which 3 were waited for; matrix products, arithmetic and copies ran while one was open for 0% of the time, Pallas kernels for 0%

profile of v2, /device:TPU:1, one launch (start us, length us, event | category | flops | bytes accessed | tf_op | source)
XLA Modules:
  0.0 242.8 jit_solution(14756257692388837000)
XLA Ops:
  2.1 1.6 fusion.65
  3.7 1.5 fusion.72
  5.2 2.0 fusion.66
  7.2 2.7 %fusion.28 = f32[512,512]{1,0:T(8,128)S(1)} fusion(bf16[1,1,2,512,512]{4,3,2,1,0:T(8,128)(2,1)} %param.9, f32[2,512,512]{2,1,0:T(8,128)} %fusion.66, pred[2]{0:T(512)(128)(4,1)S(1)} %get-tuple-element.64), kind=kOutput, calls=%fused_computation.52 | convolution fusion | flops 538181632 | bytes 4194306 | tf_op jit(solution)/shard_map/sij,sik->jk/dot_general | solution.py:105
  11.0 1.4 fusion.32
  12.3 8.7 %collective-permute-start.1 = (f32[512,512]{1,0:T(8,128)}, f32[512,512]{1,0:T(8,128)}, u32[]{:S(2)}, u32[]{:S(2)}) collective-permute-start(f32[512,512]{1,0:T(8,128)} %fusion.32), channel_id=1, source_target_pairs={{0,1},{1,0},{2,3},{3,2},{4,5},{5,4},{6,7},{7,6},{8,9},{9,8},{10,11... | collective-permute-start | bytes 3145736 | tf_op jit(solution)/shard_map/ppermute | solution.py:12
  21.1 2.6 %collective-permute-done.1 = f32[512,512]{1,0:T(8,128)} collective-permute-done((f32[512,512]{1,0:T(8,128)}, f32[512,512]{1,0:T(8,128)}, u32[]{:S(2)}, u32[]{:S(2)}) %collective-permute-start.1) | collective-permute-done | bytes 1048608 | tf_op jit(solution)/shard_map/ppermute | solution.py:12
  23.7 1.6 fusion.34
  25.3 16.6 %all_to_all.20 = f32[4,128,512]{2,1,0:T(8,128)S(1)} all-to-all(f32[4,128,512]{2,1,0:T(8,128)S(1)} %bitcast.90), channel_id=1, replica_groups=mesh['col'=8,'y'=8,'x'=4,'core'=2] {'x'}, dimensions={0} | all-to-all | bytes 2097152 | tf_op jit(solution)/shard_map/all_to_all | solution.py:18
  42.0 12.0 %all_to_all.21 = f32[8,16,512]{2,1,0:T(8,128)S(1)} all-to-all(f32[8,16,512]{2,1,0:T(8,128)S(1)} %bitcast.93), channel_id=1, replica_groups=mesh['col'=8,'y'=8,'x'=4,'core'=2] {'y'}, dimensions={0} | all-to-all | bytes 524288 | tf_op jit(solution)/shard_map/all_to_all | solution.py:18
  54.0 11.9 %all_to_all.22 = f32[8,16,512]{2,1,0:T(8,128)S(1)} all-to-all(f32[8,16,512]{2,1,0:T(8,128)S(1)} %broadcast_in_dim.49), channel_id=1, replica_groups=mesh['col'=8,'y'=8,'x'=4,'core'=2] {'y'}, dimensions={0} | all-to-all | bytes 524288 | tf_op jit(solution)/shard_map/all_to_all | solution.py:24
  66.1 13.1 %all_to_all.23 = f32[4,128,512]{2,1,0:T(8,128)S(1)} all-to-all(f32[4,128,512]{2,1,0:T(8,128)S(1)} %broadcast_in_dim.51), channel_id=1, replica_groups=mesh['col'=8,'y'=8,'x'=4,'core'=2] {'x'}, dimensions={0} | all-to-all | bytes 2097152 | tf_op jit(solution)/shard_map/all_to_all | solution.py:24
  79.2 7.2 %collective-permute-start.2 = (f32[512,512]{1,0:T(8,128)S(1)}, f32[512,512]{1,0:T(8,128)}, u32[]{:S(2)}, u32[]{:S(2)}) collective-permute-start(f32[512,512]{1,0:T(8,128)S(1)} %bitcast.91), channel_id=1, source_target_pairs={{0,1},{1,0},{2,3},{3,2},{4,5},{5,4},{6,7},{7,6},{8,9},{9,8},{10,11... | collective-permute-start | bytes 3145736 | tf_op jit(solution)/shard_map/ppermute | solution.py:12
  86.8 2.0 collective-permute-done.2
  88.9 1.3 constant_dynamic-update-slice_fusion
  91.5 2.0 fusion.35
  93.5 2.5 %copy.39 = f32[512,512]{0,1:T(8,128)} copy(f32[512,512]{1,0:T(8,128)} %fusion.35) | data formatting | bytes 2097152 | tf_op jit(solution)/shard_map/dot_general | solution.py:114
  96.0 2.5 %fusion.63 = f32[512,512]{1,0:T(8,128)S(1)} fusion(f32[512,512]{1,0:T(8,128)} %fusion.35, f32[512,512]{0,1:T(8,128)} %copy.39, bf16[1,512,512]{2,1,0:T(8,128)(2,1)S(1)} %copy-done.3), kind=kOutput, calls=%fused_computation.89 | convolution fusion | flops 1611137024 | bytes 3670016 | tf_op jit(solution)/shard_map/dot_general | solution.py:117
  98.5 2.1 convolution_multiply_fusion
  100.6 43.8 %while.10 = (s32[]{:T(128)}, f32[1280,128]{1,0:T(8,128)S(1)}, f32[512,512]{1,0:T(8,128)S(1)}, f32[512,512]{1,0:T(8,128)}, s32[]{:T(128)}) while((s32[]{:T(128)}, f32[1280,128]{1,0:T(8,128)S(1)}, f32[512,512]{1,0:T(8,128)S(1)}, f32[512,512]{1,0:T(8,128)}, s32[]{:T(128)}) %tuple.56), condition=%wide.region_4.5_spmd, body=%wide.region_3.4_spmd.sunk | while | flops 1614217216 | bytes 19923072 | solution.py:129
  102.8 2.1 fusion.102
  109.1 2.1 fusion.102
  115.3 2.1 fusion.102
  121.6 2.1 fusion.102
  127.8 2.1 fusion.102
  134.1 2.1 fusion.102
  140.3 2.1 fusion.102
  144.4 1.3 collective-permute-start.3
  145.8 90.4 %collective-permute-done.3 = f32[1280,128]{1,0:T(8,128)S(1)} collective-permute-done((f32[1280,128]{1,0:T(8,128)S(1)}, f32[1280,128]{1,0:T(8,128)S(1)}, u32[]{:S(2)}, u32[]{:S(2)}) %collective-permute-start.3) | collective-permute-done | bytes 655392 | tf_op jit(solution)/shard_map/ppermute | solution.py:130
  237.0 2.4 broadcast_multiply_fusion
  239.4 1.9 fusion.29
  241.2 1.6 fusion.31
  (187 shorter events, 32.0 us)
Async XLA Ops:
  0.6 4.5 %copy-start = (bf16[1,1,2,512,512]{4,3,2,1,0:T(8,128)(2,1)S(1)}, bf16[1,1,2,512,512]{4,3,2,1,0:T(8,128)(2,1)}, u32[]{:S(2)}) copy-start(bf16[1,1,2,512,512]{4,3,2,1,0:T(8,128)(2,1)} %param.10) | copy-start | bytes 3145732
  0.6 4.5 %copy-start.3 = (bf16[1,512,512]{2,1,0:T(8,128)(2,1)S(1)}, bf16[1,512,512]{2,1,0:T(8,128)(2,1)}, u32[]{:S(2)}) copy-start(bf16[1,512,512]{2,1,0:T(8,128)(2,1)} %param.12) | copy-start | bytes 1572868
  7.2 2.7 %copy-start.7 = (f32[1,8,512]{2,1,0:T(8,128)S(1)}, f32[1,8,512]{2,1,0:T(8,128)}, u32[]{:S(2)}) copy-start(f32[1,8,512]{2,1,0:T(8,128)} %param.13) | copy-start | bytes 49156
  10.0 1.0 copy-start.5
  12.3 11.3 %collective-permute-start.1 = (f32[512,512]{1,0:T(8,128)}, f32[512,512]{1,0:T(8,128)}, u32[]{:S(2)}, u32[]{:S(2)}) collective-permute-start(f32[512,512]{1,0:T(8,128)} %fusion.32), channel_id=1, source_target_pairs={{0,1},{1,0},{2,3},{3,2},{4,5},{5,4},{6,7},{7,6},{8,9},{9,8},{10,11... | collective-permute-start | bytes 3145736 | tf_op jit(solution)/shard_map/ppermute | solution.py:12
  79.2 9.6 %collective-permute-start.2 = (f32[512,512]{1,0:T(8,128)S(1)}, f32[512,512]{1,0:T(8,128)}, u32[]{:S(2)}, u32[]{:S(2)}) collective-permute-start(f32[512,512]{1,0:T(8,128)S(1)} %bitcast.91), channel_id=1, source_target_pairs={{0,1},{1,0},{2,3},{3,2},{4,5},{5,4},{6,7},{7,6},{8,9},{9,8},{10,11... | collective-permute-start | bytes 3145736 | tf_op jit(solution)/shard_map/ppermute | solution.py:12
  86.8 4.7 %copy-start.6 = (bf16[1,512,512]{2,1,0:T(8,128)(2,1)S(1)}, bf16[1,512,512]{2,1,0:T(8,128)(2,1)}, u32[]{:S(2)}) copy-start(bf16[1,512,512]{2,1,0:T(8,128)(2,1)} %param.11) | copy-start | bytes 1572868
  90.2 1.3 copy-start.4
  102.8 2.1 copy-start.1
  106.2 0.7 collective-permute-start
  109.0 2.1 copy-start.1
  112.4 0.7 collective-permute-start
  115.3 2.1 copy-start.1
  118.7 0.7 collective-permute-start
  121.6 2.1 copy-start.1
  124.9 0.7 collective-permute-start
  127.8 2.1 copy-start.1
  131.2 0.7 collective-permute-start
  134.1 2.1 copy-start.1
  137.5 0.7 collective-permute-start
  140.3 2.1 copy-start.1
  143.7 0.7 collective-permute-start
  144.4 91.7 %collective-permute-start.3 = (f32[1280,128]{1,0:T(8,128)S(1)}, f32[1280,128]{1,0:T(8,128)S(1)}, u32[]{:S(2)}, u32[]{:S(2)}) collective-permute-start(f32[1280,128]{1,0:T(8,128)S(1)} %get-tuple-element.24), channel_id=1, source_target_pairs={{0,1},{2,3},{4,5},{6,7},{8,9},{10,11},{12,13},{14,15},{16,17},{18,... | collective-permute-start | bytes 1966088 | tf_op jit(solution)/shard_map/ppermute | solution.py:130
  237.0 4.2 %copy-start.2 = (f32[2,512,512]{2,1,0:T(8,128)S(1)}, f32[2,512,512]{2,1,0:T(8,128)}, u32[]{:S(2)}) copy-start(f32[2,512,512]{2,1,0:T(8,128)} %fusion.66) | copy-start | bytes 6291460

commit v3 on v2

--- a/solution.py
+++ b/solution.py
@@ -82,7 +82,6 @@
 def on_device(
     panel_factor, panel_cotangent, diag_factor, diag_inverse, diag_cotangent, tile_count, tile_rows
 ):
-    full = lax.Precision.HIGHEST
     chain = lax.Precision.HIGH
     factors = panel_factor[0, 0]
     cotangent = panel_cotangent[0, 0]
@@ -111,22 +110,20 @@
     summed = reduced[:width]
     link_wide = reduced[width:]
     inverse_wide = inverse.astype(jnp.float32)
-    curvature = jnp.dot(lower.astype(jnp.float32).T, summed, precision=full)
+    curvature = jnp.dot(lower.astype(jnp.float32).T, summed, precision=chain)
     symmetric = symmetrize(curvature)
     own_map = 0.5 * jnp.dot(
-        inverse_wide.T, jnp.dot(symmetric, inverse_wide, precision=full), precision=full
+        inverse_wide.T, jnp.dot(symmetric, inverse_wide, precision=chain), precision=chain
     )
     down = [(2 * i, 2 * (i - 1)) for i in range(1, groups)]
 
-    def sweep(_, packed):
+    packed = lax.ppermute(pack(own_map), ("col", "core"), down)
+    for _ in range(groups - 2):
         incoming = unpack(packed, width)
         advanced = own_map + jnp.dot(
             link_wide.T, jnp.dot(incoming, link_wide, precision=chain), precision=chain
         )
-        return lax.ppermute(pack(advanced), ("col", "core"), down)
-
-    start = jnp.zeros((BLOCKS * (BLOCKS + 1) // 2 * width // BLOCKS, width // BLOCKS), jnp.float32)
-    packed = lax.fori_loop(0, groups - 1, sweep, start)
+        packed = lax.ppermute(pack(advanced), ("col", "core"), down)
     shared = lax.ppermute(packed, "core", [(0, 1)])
     incoming = unpack(jnp.where(core == 0, packed, shared), width)
     product = jnp.dot(incoming, link_wide, precision=chain)

time: 246 us -> 308 us (1.25)
  local copies, waits for them, and re-layouts: 22.5 us -> 74.1 us
  other arithmetic: 7.17 us -> 14.4 us
    unnamed x19 -> x111, local copies, waits for them, and re-layouts: 2.71 us -> 55.5 us
    concatenate x8 -> x7, other arithmetic: 0.16 us -> 5.74 us  [unpack(): jnp.concatenate([blocks[i, j] if i >= j else blocks[j, i].T for j in rang...]
    transpose x7 -> x0, local copies, waits for them, and re-layouts: 4.94 us -> none  [unpack(): blocks[j, i]]
    concatenate x8 -> x7, local copies, waits for them, and re-layouts: 1.03 us -> 5.86 us  [unpack(): jnp.concatenate([blocks[i, j] if i >= j else blocks[j, i].T for j in rang...]
    concatenate x7, local copies, waits for them, and re-layouts: 0.08 us -> 4.47 us  [pack(): jnp.concatenate([matrix[i * size:(i + 1) * size, j * size:(j + 1) * size]...]
    dot_general x17 -> x15, matrix products: 28.8 us -> 30.5 us  [the longest x6 13.7 us: on_device(): jnp.dot(link_wide.T, jnp.dot(incoming, link_wide, precision=chain), preci...]
    slice x29 -> x7, local copies, waits for them, and re-layouts: 7.09 us -> 5.41 us  [unpack(): blocks[i, j] = packed[k * size:(k + 1) * size]]
where the time goes in v3:
time: 308 us; the launch traced here: 304 us
  waiting for transfers between devices  94.7 us (31%)
  local copies, waits for them, and re-layouts  74.1 us (24%)
  blocking collectives  54.6 us (18%)
  matrix products  42.1 us (14%)
  starting transfers between devices  22.1 us (7%)
  other arithmetic  14.4 us (5%)
    ppermute x1, waiting for transfers between devices, on_device(): shared = lax.ppermute(packed, 'core', [(0, 1)])  90.1 us
    unnamed x111, local copies, waits for them, and re-layouts  55.5 us
    all_to_all x2, blocking collectives, scatter_sum(): return jnp.sum(lax.all_to_all(pieces, axis, 0, 0), axis=0)  29.6 us
    all_to_all x2, blocking collectives, gather_all(): gathered = lax.all_to_all(spread, axis, 0, 0)  25 us
    ppermute x2, starting transfers between devices, swap_cores(): return lax.ppermute(value, 'core', [(0, 1), (1, 0)])  14.7 us
    dot_general x6, matrix products, on_device(): jnp.dot(link_wide.T, jnp.dot(incoming, link_wide, precision=chain), preci...  13.7 us
    dot_general x6, matrix products, on_device(): jnp.dot(incoming, link_wide, precision=chain)  13.4 us
  transfers between devices with their start and end apart: 10, of which 3 were waited for; matrix products, arithmetic and copies ran while one was open for 0% of the time, Pallas kernels for 0%

profile of v3, /device:TPU:1, one launch (start us, length us, event | category | flops | bytes accessed | tf_op | source)
XLA Modules:
  0.0 304.1 jit_solution(12797269225688986661)
XLA Ops:
  1.9 3.2 %fusion.194 = f32[2,512,512]{2,1,0:T(8,128)} fusion(bf16[1,1,2,512,512]{4,3,2,1,0:T(8,128)(2,1)S(1)} %copy-done, bf16[1,512,512]{2,1,0:T(8,128)(2,1)} %param.10), kind=kOutput, calls=%fused_computation.210 | convolution fusion | flops 536870912 | bytes 3670016 | tf_op jit(solution)/shard_map/sij,jk->sik/dot_general | solution.py:100
  5.9 3.6 %fusion = f32[512,512]{1,0:T(8,128)} fusion(bf16[1,1,2,512,512]{4,3,2,1,0:T(8,128)(2,1)} %param.7, f32[2,512,512]{2,1,0:T(8,128)} %fusion.194, pred[2]{0:T(512)(128)(4,1)S(1)} %get-tuple-element.89), kind=kOutput, calls=%fused_computation.13 | convolution fusion | flops 538181632 | bytes 4194306 | tf_op jit(solution)/shard_map/sij,sik->jk/dot_general | solution.py:104
  10.9 2.5 fusion.4
  13.4 7.5 %collective-permute-start = (f32[512,512]{1,0:T(8,128)}, f32[512,512]{1,0:T(8,128)}, u32[]{:S(2)}, u32[]{:S(2)}) collective-permute-start(f32[512,512]{1,0:T(8,128)} %fusion.4), channel_id=1, source_target_pairs={{0,1},{1,0},{2,3},{3,2},{4,5},{5,4},{6,7},{7,6},{8,9},{9,8},{10,11... | collective-permute-start | bytes 3145736 | tf_op jit(solution)/shard_map/ppermute | solution.py:12
  20.9 2.6 collective-permute-done
  23.5 1.6 fusion.6
  25.1 16.6 %all_to_all.20 = f32[4,128,512]{2,1,0:T(8,128)S(1)} all-to-all(f32[4,128,512]{2,1,0:T(8,128)S(1)} %bitcast.128), channel_id=1, replica_groups=mesh['col'=8,'y'=8,'x'=4,'core'=2] {'x'}, dimensions={0} | all-to-all | bytes 2097152 | tf_op jit(solution)/shard_map/all_to_all | solution.py:18
  41.9 13.0 %all_to_all.21 = f32[8,16,512]{2,1,0:T(8,128)S(1)} all-to-all(f32[8,16,512]{2,1,0:T(8,128)S(1)} %bitcast.131), channel_id=1, replica_groups=mesh['col'=8,'y'=8,'x'=4,'core'=2] {'y'}, dimensions={0} | all-to-all | bytes 524288 | tf_op jit(solution)/shard_map/all_to_all | solution.py:18
  54.9 11.8 %all_to_all.22 = f32[8,16,512]{2,1,0:T(8,128)S(1)} all-to-all(f32[8,16,512]{2,1,0:T(8,128)S(1)} %broadcast_in_dim.45), channel_id=1, replica_groups=mesh['col'=8,'y'=8,'x'=4,'core'=2] {'y'}, dimensions={0} | all-to-all | bytes 524288 | tf_op jit(solution)/shard_map/all_to_all | solution.py:24
  66.8 13.1 %all_to_all.23 = f32[4,128,512]{2,1,0:T(8,128)S(1)} all-to-all(f32[4,128,512]{2,1,0:T(8,128)S(1)} %broadcast_in_dim.47), channel_id=1, replica_groups=mesh['col'=8,'y'=8,'x'=4,'core'=2] {'x'}, dimensions={0} | all-to-all | bytes 2097152 | tf_op jit(solution)/shard_map/all_to_all | solution.py:24
  80.0 7.2 %collective-permute-start.1 = (f32[512,512]{1,0:T(8,128)S(1)}, f32[512,512]{1,0:T(8,128)S(1)}, u32[]{:S(2)}, u32[]{:S(2)}) collective-permute-start(f32[512,512]{1,0:T(8,128)S(1)} %bitcast.129), channel_id=1, source_target_pairs={{0,1},{1,0},{2,3},{3,2},{4,5},{5,4},{6,7},{7,6},{8,9},{9,8},{10,11... | collective-permute-start | bytes 3145736 | tf_op jit(solution)/shard_map/ppermute | solution.py:12
  87.6 1.9 collective-permute-done.1
  89.6 1.3 copy-done.2
  93.0 1.9 fusion.191
  106.3 2.6 fusion.9
  108.9 2.3 convolution_add_fusion.5
  122.8 2.1 fusion.35
  125.0 2.3 convolution_add_fusion.4
  139.1 2.1 fusion.61
  141.3 2.3 convolution_add_fusion.3
  155.2 2.1 fusion.87
  157.3 2.3 convolution_add_fusion.2
  171.3 2.1 fusion.113
  173.4 2.3 convolution_add_fusion.1
  187.4 2.1 fusion.139
  189.5 2.3 convolution_add_fusion
  197.6 1.5 collective-permute-start.8
  199.1 1.5 collective-permute-start.9
  201.7 90.1 %collective-permute-done.9 = f32[1280,128]{1,0:T(8,128)} collective-permute-done((f32[1280,128]{1,0:T(8,128)}, f32[1280,128]{1,0:T(8,128)}, u32[]{:S(2)}, u32[]{:S(2)}) %collective-permute-start.9) | collective-permute-done | bytes 655392 | tf_op jit(solution)/shard_map/ppermute | solution.py:127
  298.2 2.3 broadcast_multiply_fusion
  300.4 1.6 fusion.3
  302.0 2.1 fusion.1
  (167 shorter events, 87.8 us)
Async XLA Ops:
  0.6 1.2 copy-start
  0.6 4.4 %copy-start.9 = (s32[1,1,2]{2,1,0:T(1,128)S(1)}, s32[1,1,2]{2,1,0:T(1,128)}, u32[]{:S(2)}) copy-start(s32[1,1,2]{2,1,0:T(1,128)} %param.13) | copy-start | bytes 28
  0.7 4.4 %copy-start.6 = (bf16[1,1,2,512,512]{4,3,2,1,0:T(8,128)(2,1)S(1)}, bf16[1,1,2,512,512]{4,3,2,1,0:T(8,128)(2,1)}, u32[]{:S(2)}) copy-start(bf16[1,1,2,512,512]{4,3,2,1,0:T(8,128)(2,1)} %param.7) | copy-start | bytes 3145732
  1.9 3.6 %copy-start.5 = (bf16[1,512,512]{2,1,0:T(8,128)(2,1)S(1)}, bf16[1,512,512]{2,1,0:T(8,128)(2,1)}, u32[]{:S(2)}) copy-start(bf16[1,512,512]{2,1,0:T(8,128)(2,1)} %param.10) | copy-start | bytes 1572868
  5.9 3.7 %copy-start.8 = (f32[1,8,512]{2,1,0:T(8,128)S(1)}, f32[1,8,512]{2,1,0:T(8,128)}, u32[]{:S(2)}) copy-start(f32[1,8,512]{2,1,0:T(8,128)} %param.11) | copy-start | bytes 49156
  13.4 10.1 %collective-permute-start = (f32[512,512]{1,0:T(8,128)}, f32[512,512]{1,0:T(8,128)}, u32[]{:S(2)}, u32[]{:S(2)}) collective-permute-start(f32[512,512]{1,0:T(8,128)} %fusion.4), channel_id=1, source_target_pairs={{0,1},{1,0},{2,3},{3,2},{4,5},{5,4},{6,7},{7,6},{8,9},{9,8},{10,11... | collective-permute-start | bytes 3145736 | tf_op jit(solution)/shard_map/ppermute | solution.py:12
  80.0 9.5 %collective-permute-start.1 = (f32[512,512]{1,0:T(8,128)S(1)}, f32[512,512]{1,0:T(8,128)S(1)}, u32[]{:S(2)}, u32[]{:S(2)}) collective-permute-start(f32[512,512]{1,0:T(8,128)S(1)} %bitcast.129), channel_id=1, source_target_pairs={{0,1},{1,0},{2,3},{3,2},{4,5},{5,4},{6,7},{7,6},{8,9},{9,8},{10,11... | collective-permute-start | bytes 3145736 | tf_op jit(solution)/shard_map/ppermute | solution.py:12
  87.5 3.5 %copy-start.7 = (bf16[1,512,512]{2,1,0:T(8,128)(2,1)S(1)}, bf16[1,512,512]{2,1,0:T(8,128)(2,1)}, u32[]{:S(2)}) copy-start(bf16[1,512,512]{2,1,0:T(8,128)(2,1)} %param.9) | copy-start | bytes 1572868
  89.6 1.4 copy-start.2
  95.7 9.1 %copy-start.1 = (f32[512,512]{0,1:T(8,128)}, f32[512,512]{0,1:T(8,128)S(1)}, u32[]{:S(2)}) copy-start(f32[512,512]{0,1:T(8,128)S(1)} %convolution_multiply_fusion) | copy-start | bytes 3145732
  101.6 0.7 collective-permute-start.2
  106.3 2.6 copy-start.3
  117.0 0.7 collective-permute-start.3
  133.1 0.9 collective-permute-start.4
  149.3 0.7 collective-permute-start.5
  165.4 0.7 collective-permute-start.6
  181.5 0.7 collective-permute-start.7
  197.6 1.5 collective-permute-start.8
  199.1 92.7 %collective-permute-start.9 = (f32[1280,128]{1,0:T(8,128)}, f32[1280,128]{1,0:T(8,128)}, u32[]{:S(2)}, u32[]{:S(2)}) collective-permute-start(f32[1280,128]{1,0:T(8,128)} %collective-permute-done.8), channel_id=1, source_target_pairs={{0,1},{2,3},{4,5},{6,7},{8,9},{10,11},{12,13},{14,15},{16,17},{18,... | collective-permute-start | bytes 1966088 | tf_op jit(solution)/shard_map/ppermute | solution.py:127
  298.1 2.3 copy-start.4

commit v4 on v2

--- a/solution.py
+++ b/solution.py
@@ -35,10 +35,7 @@
         mine = scatter_sum(mine, axis)
     for axis in CHIPS:
         mine = gather_all(mine, axis)
-    other = swap_cores(mine)
-    whole = jnp.zeros(value.shape, value.dtype)
-    whole = lax.dynamic_update_slice_in_dim(whole, mine, core * half, 0)
-    return lax.dynamic_update_slice_in_dim(whole, other, (1 - core) * half, 0)
+    return mine
 
 
 BLOCKS = 4
@@ -82,7 +79,6 @@
 def on_device(
     panel_factor, panel_cotangent, diag_factor, diag_inverse, diag_cotangent, tile_count, tile_rows
 ):
-    full = lax.Precision.HIGHEST
     chain = lax.Precision.HIGH
     factors = panel_factor[0, 0]
     cotangent = panel_cotangent[0, 0]
@@ -107,26 +103,31 @@
     panel_terms = lax.dynamic_update_slice_in_dim(panel_terms, own_rows, row_start, 0)
     chosen = jnp.sum(jnp.where(link_flag[:, None, None], factors, jnp.zeros_like(factors)), axis=0)
     link_part = jnp.dot(chosen, inverse, preferred_element_type=jnp.float32)
-    reduced = all_sum(jnp.concatenate([panel_terms, link_part], axis=0))
-    summed = reduced[:width]
-    link_wide = reduced[width:]
+    mine = all_sum(jnp.concatenate([panel_terms, link_part], axis=0))
+    other = swap_cores(mine)
+    link_wide = jnp.where(core == 0, other, mine)
     inverse_wide = inverse.astype(jnp.float32)
-    curvature = jnp.dot(lower.astype(jnp.float32).T, summed, precision=full)
-    symmetric = symmetrize(curvature)
-    own_map = 0.5 * jnp.dot(
-        inverse_wide.T, jnp.dot(symmetric, inverse_wide, precision=full), precision=full
-    )
+    lower_wide = lower.astype(jnp.float32)
+
+    def own_of(summed):
+        symmetric = symmetrize(jnp.dot(lower_wide.T, summed, precision=chain))
+        return 0.5 * jnp.dot(
+            inverse_wide.T, jnp.dot(symmetric, inverse_wide, precision=chain), precision=chain
+        )
+
+    chain_own = own_of(mine)
     down = [(2 * i, 2 * (i - 1)) for i in range(1, groups)]
 
     def sweep(_, packed):
         incoming = unpack(packed, width)
-        advanced = own_map + jnp.dot(
+        advanced = chain_own + jnp.dot(
             link_wide.T, jnp.dot(incoming, link_wide, precision=chain), precision=chain
         )
         return lax.ppermute(pack(advanced), ("col", "core"), down)
 
-    start = jnp.zeros((BLOCKS * (BLOCKS + 1) // 2 * width // BLOCKS, width // BLOCKS), jnp.float32)
-    packed = lax.fori_loop(0, groups - 1, sweep, start)
+    first = lax.ppermute(pack(chain_own), ("col", "core"), down)
+    packed = lax.fori_loop(0, groups - 2, sweep, first)
+    own_map = jnp.where(core == 0, chain_own, own_of(other))
     shared = lax.ppermute(packed, "core", [(0, 1)])
     incoming = unpack(jnp.where(core == 0, packed, shared), width)
     product = jnp.dot(incoming, link_wide, precision=chain)

time: 246 us -> 275 us (1.12)
  the two profiles are of different devices: /device:TPU:1 before, /device:TPU:192 now
where the time goes in v4:
time: 275 us; the launch traced here: 273 us
  waiting for transfers between devices  82.9 us (30%)
  blocking collectives  64.5 us (23%)
  local copies, waits for them, and re-layouts  46.5 us (17%)
  matrix products  42.2 us (15%)
  starting transfers between devices  19.5 us (7%)
  other arithmetic  15.4 us (6%)
    ppermute x6, waiting for transfers between devices, sweep(): return lax.ppermute(pack(advanced), ('col', 'core'), down)  70.5 us
    all_to_all x2, blocking collectives, scatter_sum(): return jnp.sum(lax.all_to_all(pieces, axis, 0, 0), axis=0)  36.8 us
    all_to_all x2, blocking collectives, gather_all(): gathered = lax.all_to_all(spread, axis, 0, 0)  27.7 us
    slice x25, local copies, waits for them, and re-layouts, unpack(): blocks[i, j] = packed[k * size:(k + 1) * size]  17.9 us
    dot_general x6, matrix products, sweep(): jnp.dot(incoming, link_wide, precision=chain)  13.7 us
    ppermute x6, starting transfers between devices, sweep(): return lax.ppermute(pack(advanced), ('col', 'core'), down)  11.5 us
    transpose x6, local copies, waits for them, and re-layouts, unpack(): blocks[j, i]  10.7 us
    ppermute x1, waiting for transfers between devices, on_device(): first = lax.ppermute(pack(chain_own), ('col', 'core'), down)  9.35 us
  transfers between devices with their start and end apart: 10, of which 8 were waited for; matrix products, arithmetic and copies ran while one was open for 7% of the time, Pallas kernels for 0%

profile of v4, /device:TPU:192, one launch (start us, length us, event | category | flops | bytes accessed | tf_op | source)
XLA Modules:
  0.0 273.4 jit_solution(4044353081139846371)
XLA Ops:
  5.2 2.0 fusion.67
  7.2 2.7 fusion.30
  14.2 3.0 %collective-permute-done.1 = f32[512,512]{1,0:T(8,128)} collective-permute-done((f32[512,512]{1,0:T(8,128)}, f32[512,512]{1,0:T(8,128)}, u32[]{:S(2)}, u32[]{:S(2)}) %collective-permute-start.1) | collective-permute-done | bytes 1048608 | tf_op jit(solution)/shard_map/ppermute | solution.py:12
  17.2 1.9 fusion.36
  19.1 19.2 %all_to_all.20 = f32[4,128,512]{2,1,0:T(8,128)S(1)} all-to-all(f32[4,128,512]{2,1,0:T(8,128)S(1)} %bitcast.103), channel_id=1, replica_groups=mesh['col'=8,'y'=8,'x'=4,'core'=2] {'x'}, dimensions={0} | all-to-all | bytes 2097152 | tf_op jit(solution)/shard_map/all_to_all | solution.py:18
  38.4 17.6 %all_to_all.21 = f32[8,16,512]{2,1,0:T(8,128)S(1)} all-to-all(f32[8,16,512]{2,1,0:T(8,128)S(1)} %bitcast.104), channel_id=1, replica_groups=mesh['col'=8,'y'=8,'x'=4,'core'=2] {'y'}, dimensions={0} | all-to-all | bytes 524288 | tf_op jit(solution)/shard_map/all_to_all | solution.py:18
  56.1 13.0 %all_to_all.22 = f32[8,16,512]{2,1,0:T(8,128)S(1)} all-to-all(f32[8,16,512]{2,1,0:T(8,128)S(1)} %broadcast_in_dim.41), channel_id=1, replica_groups=mesh['col'=8,'y'=8,'x'=4,'core'=2] {'y'}, dimensions={0} | all-to-all | bytes 524288 | tf_op jit(solution)/shard_map/all_to_all | solution.py:24
  69.2 14.7 %all_to_all.23 = f32[4,128,512]{2,1,0:T(8,128)} all-to-all(f32[4,128,512]{2,1,0:T(8,128)S(1)} %broadcast_in_dim.43), channel_id=1, replica_groups=mesh['col'=8,'y'=8,'x'=4,'core'=2] {'x'}, dimensions={0} | all-to-all | bytes 2097152 | tf_op jit(solution)/shard_map/all_to_all | solution.py:24
  85.8 2.0 fusion.72
  89.1 1.9 fusion.64
  94.0 2.7 %broadcast_select_fusion = f32[512,512]{1,0:T(8,128)} fusion(f32[512,512]{1,0:T(8,128)} %collective-permute-done.3, pred[]{:T(512)S(6)} %eq.21, f32[4,128,512]{2,1,0:T(8,128)} %all_to_all.23), kind=kLoop, calls=%fused_computation.114 | loop fusion | flops 262144 | bytes 3145729 | tf_op jit(solution)/shard_map/jit(_where)/select_n | solution.py:108
  96.7 9.4 %collective-permute-done.2 = f32[1280,128]{1,0:T(8,128)S(1)} collective-permute-done((f32[1280,128]{1,0:T(8,128)S(1)}, f32[1280,128]{1,0:T(8,128)S(1)}, u32[]{:S(2)}, u32[]{:S(2)}) %collective-permute-start.2) | collective-permute-done | bytes 655392 | tf_op jit(solution)/shard_map/ppermute | solution.py:128
  106.1 148.6 %while.10 = (s32[]{:T(128)}, f32[1280,128]{1,0:T(8,128)S(1)}, f32[512,512]{1,0:T(8,128)}, f32[512,512]{1,0:T(8,128)S(1)}, s32[]{:T(128)}) while((s32[]{:T(128)}, f32[1280,128]{1,0:T(8,128)S(1)}, f32[512,512]{1,0:T(8,128)}, f32[512,512]{1,0:T(8,128)S(1)}, s32[]{:T(128)}) %tuple.53), condition=%wide.region_4.5_spmd, body=%wide.region_3.4_spmd.sunk | while | flops 1614217216 | bytes 19923072 | solution.py:129
  113.7 2.3 fusion.111
  117.2 1.9 collective-permute-start
  119.1 11.8 %collective-permute-done = f32[1280,128]{1,0:T(8,128)S(1)} collective-permute-done((f32[1280,128]{1,0:T(8,128)S(1)}, f32[1280,128]{1,0:T(8,128)S(1)}, u32[]{:S(2)}, u32[]{:S(2)}) %collective-permute-start) | collective-permute-done | bytes 655392 | tf_op jit(solution)/shard_map/while/body/eval_jaxpr/ppermute | solution.py:126
  138.4 2.3 fusion.111
  143.8 11.8 %collective-permute-done = f32[1280,128]{1,0:T(8,128)S(1)} collective-permute-done((f32[1280,128]{1,0:T(8,128)S(1)}, f32[1280,128]{1,0:T(8,128)S(1)}, u32[]{:S(2)}, u32[]{:S(2)}) %collective-permute-start) | collective-permute-done | bytes 655392 | tf_op jit(solution)/shard_map/while/body/eval_jaxpr/ppermute | solution.py:126
  163.2 2.3 fusion.111
  168.6 11.8 %collective-permute-done = f32[1280,128]{1,0:T(8,128)S(1)} collective-permute-done((f32[1280,128]{1,0:T(8,128)S(1)}, f32[1280,128]{1,0:T(8,128)S(1)}, u32[]{:S(2)}, u32[]{:S(2)}) %collective-permute-start) | collective-permute-done | bytes 655392 | tf_op jit(solution)/shard_map/while/body/eval_jaxpr/ppermute | solution.py:126
  187.9 2.3 fusion.111
  193.4 11.8 %collective-permute-done = f32[1280,128]{1,0:T(8,128)S(1)} collective-permute-done((f32[1280,128]{1,0:T(8,128)S(1)}, f32[1280,128]{1,0:T(8,128)S(1)}, u32[]{:S(2)}, u32[]{:S(2)}) %collective-permute-start) | collective-permute-done | bytes 655392 | tf_op jit(solution)/shard_map/while/body/eval_jaxpr/ppermute | solution.py:126
  212.7 2.3 fusion.111
  218.1 11.8 %collective-permute-done = f32[1280,128]{1,0:T(8,128)S(1)} collective-permute-done((f32[1280,128]{1,0:T(8,128)S(1)}, f32[1280,128]{1,0:T(8,128)S(1)}, u32[]{:S(2)}, u32[]{:S(2)}) %collective-permute-start) | collective-permute-done | bytes 655392 | tf_op jit(solution)/shard_map/while/body/eval_jaxpr/ppermute | solution.py:126
  237.5 2.3 fusion.111
  242.9 11.8 %collective-permute-done = f32[1280,128]{1,0:T(8,128)S(1)} collective-permute-done((f32[1280,128]{1,0:T(8,128)S(1)}, f32[1280,128]{1,0:T(8,128)S(1)}, u32[]{:S(2)}, u32[]{:S(2)}) %collective-permute-start) | collective-permute-done | bytes 655392 | tf_op jit(solution)/shard_map/while/body/eval_jaxpr/ppermute | solution.py:126
  254.6 2.3 collective-permute-start.4
  256.9 3.1 %fusion.70 = f32[512,512]{1,0:T(8,128)} fusion(f32[512,512]{1,0:T(8,128)} %collective-permute-done.3, bf16[1,512,512]{2,1,0:T(8,128)(2,1)} %param.11), kind=kOutput, calls=%fused_computation.101 | convolution fusion | flops 805306368 | bytes 2621440 | tf_op jit(solution)/shard_map/dot_general | solution.py:113
  260.0 2.5 copy.50
  262.5 2.3 fusion.63
  267.4 2.4 broadcast_multiply_fusion
  271.4 2.1 fusion.31
  (175 shorter events, 80.2 us)
Async XLA Ops:
  0.6 4.5 %copy-start = (bf16[1,1,2,512,512]{4,3,2,1,0:T(8,128)(2,1)S(1)}, bf16[1,1,2,512,512]{4,3,2,1,0:T(8,128)(2,1)}, u32[]{:S(2)}) copy-start(bf16[1,1,2,512,512]{4,3,2,1,0:T(8,128)(2,1)} %param.10) | copy-start | bytes 3145732
  0.6 4.5 %copy-start.2 = (bf16[1,512,512]{2,1,0:T(8,128)(2,1)S(1)}, bf16[1,512,512]{2,1,0:T(8,128)(2,1)}, u32[]{:S(2)}) copy-start(bf16[1,512,512]{2,1,0:T(8,128)(2,1)} %param.12) | copy-start | bytes 1572868
  7.2 2.7 copy-start.7
  9.9 1.0 copy-start.5
  12.3 4.9 %collective-permute-start.1 = (f32[512,512]{1,0:T(8,128)}, f32[512,512]{1,0:T(8,128)}, u32[]{:S(2)}, u32[]{:S(2)}) collective-permute-start(f32[512,512]{1,0:T(8,128)} %fusion.34), channel_id=1, source_target_pairs={{0,1},{1,0},{2,3},{3,2},{4,5},{5,4},{6,7},{7,6},{8,9},{9,8},{10,11... | collective-permute-start | bytes 3145736 | tf_op jit(solution)/shard_map/ppermute | solution.py:12
  56.0 29.8 %copy-start.6 = (bf16[1,512,512]{2,1,0:T(8,128)(2,1)S(1)}, bf16[1,512,512]{2,1,0:T(8,128)(2,1)}, u32[]{:S(2)}) copy-start(bf16[1,512,512]{2,1,0:T(8,128)(2,1)} %param.11) | copy-start | bytes 1572868
  83.9 10.1 %collective-permute-start.3 = (f32[512,512]{1,0:T(8,128)}, f32[512,512]{1,0:T(8,128)}, u32[]{:S(2)}, u32[]{:S(2)}) collective-permute-start(f32[512,512]{1,0:T(8,128)} %bitcast.18), channel_id=1, source_target_pairs={{0,1},{1,0},{2,3},{3,2},{4,5},{5,4},{6,7},{7,6},{8,9},{9,8},{10,11... | collective-permute-start | bytes 3145736 | tf_op jit(solution)/shard_map/ppermute | solution.py:12
  92.0 14.0 %collective-permute-start.2 = (f32[1280,128]{1,0:T(8,128)S(1)}, f32[1280,128]{1,0:T(8,128)S(1)}, u32[]{:S(2)}, u32[]{:S(2)}) collective-permute-start(f32[1280,128]{1,0:T(8,128)S(1)} %slice_dynamic-update-slice_fusion.10), channel_id=1, source_target_pairs={{64,0},{128,64},{192,128},{256,192},{320,256},{384,320},{448,384},... | collective-permute-start | bytes 1966088 | tf_op jit(solution)/shard_map/ppermute | solution.py:128
  108.0 5.7 %copy-start.1 = (f32[512,512]{1,0:T(8,128)S(1)}, f32[512,512]{1,0:T(8,128)}, u32[]{:S(2)}) copy-start(f32[512,512]{1,0:T(8,128)} %get-tuple-element.134) | copy-start | bytes 3145732 | tf_op jit(solution)/shard_map/while
  117.2 13.7 %collective-permute-start = (f32[1280,128]{1,0:T(8,128)S(1)}, f32[1280,128]{1,0:T(8,128)S(1)}, u32[]{:S(2)}, u32[]{:S(2)}) collective-permute-start(f32[1280,128]{1,0:T(8,128)S(1)} %slice_dynamic-update-slice_fusion.35), channel_id=1, source_target_pairs={{64,0},{128,64},{192,128},{256,192},{320,256},{384,320},{448,384},... | collective-permute-start | bytes 1966088 | tf_op jit(solution)/shard_map/while/body/eval_jaxpr/ppermute | solution.py:126
  132.7 5.7 %copy-start.1 = (f32[512,512]{1,0:T(8,128)S(1)}, f32[512,512]{1,0:T(8,128)}, u32[]{:S(2)}) copy-start(f32[512,512]{1,0:T(8,128)} %get-tuple-element.134) | copy-start | bytes 3145732 | tf_op jit(solution)/shard_map/while
  141.9 13.7 %collective-permute-start = (f32[1280,128]{1,0:T(8,128)S(1)}, f32[1280,128]{1,0:T(8,128)S(1)}, u32[]{:S(2)}, u32[]{:S(2)}) collective-permute-start(f32[1280,128]{1,0:T(8,128)S(1)} %slice_dynamic-update-slice_fusion.35), channel_id=1, source_target_pairs={{64,0},{128,64},{192,128},{256,192},{320,256},{384,320},{448,384},... | collective-permute-start | bytes 1966088 | tf_op jit(solution)/shard_map/while/body/eval_jaxpr/ppermute | solution.py:126
  157.5 5.7 %copy-start.1 = (f32[512,512]{1,0:T(8,128)S(1)}, f32[512,512]{1,0:T(8,128)}, u32[]{:S(2)}) copy-start(f32[512,512]{1,0:T(8,128)} %get-tuple-element.134) | copy-start | bytes 3145732 | tf_op jit(solution)/shard_map/while
  166.7 13.7 %collective-permute-start = (f32[1280,128]{1,0:T(8,128)S(1)}, f32[1280,128]{1,0:T(8,128)S(1)}, u32[]{:S(2)}, u32[]{:S(2)}) collective-permute-start(f32[1280,128]{1,0:T(8,128)S(1)} %slice_dynamic-update-slice_fusion.35), channel_id=1, source_target_pairs={{64,0},{128,64},{192,128},{256,192},{320,256},{384,320},{448,384},... | collective-permute-start | bytes 1966088 | tf_op jit(solution)/shard_map/while/body/eval_jaxpr/ppermute | solution.py:126
  182.2 5.7 %copy-start.1 = (f32[512,512]{1,0:T(8,128)S(1)}, f32[512,512]{1,0:T(8,128)}, u32[]{:S(2)}) copy-start(f32[512,512]{1,0:T(8,128)} %get-tuple-element.134) | copy-start | bytes 3145732 | tf_op jit(solution)/shard_map/while
  191.4 13.7 %collective-permute-start = (f32[1280,128]{1,0:T(8,128)S(1)}, f32[1280,128]{1,0:T(8,128)S(1)}, u32[]{:S(2)}, u32[]{:S(2)}) collective-permute-start(f32[1280,128]{1,0:T(8,128)S(1)} %slice_dynamic-update-slice_fusion.35), channel_id=1, source_target_pairs={{64,0},{128,64},{192,128},{256,192},{320,256},{384,320},{448,384},... | collective-permute-start | bytes 1966088 | tf_op jit(solution)/shard_map/while/body/eval_jaxpr/ppermute | solution.py:126
  207.0 5.7 %copy-start.1 = (f32[512,512]{1,0:T(8,128)S(1)}, f32[512,512]{1,0:T(8,128)}, u32[]{:S(2)}) copy-start(f32[512,512]{1,0:T(8,128)} %get-tuple-element.134) | copy-start | bytes 3145732 | tf_op jit(solution)/shard_map/while
  216.2 13.7 %collective-permute-start = (f32[1280,128]{1,0:T(8,128)S(1)}, f32[1280,128]{1,0:T(8,128)S(1)}, u32[]{:S(2)}, u32[]{:S(2)}) collective-permute-start(f32[1280,128]{1,0:T(8,128)S(1)} %slice_dynamic-update-slice_fusion.35), channel_id=1, source_target_pairs={{64,0},{128,64},{192,128},{256,192},{320,256},{384,320},{448,384},... | collective-permute-start | bytes 1966088 | tf_op jit(solution)/shard_map/while/body/eval_jaxpr/ppermute | solution.py:126
  231.8 5.7 %copy-start.1 = (f32[512,512]{1,0:T(8,128)S(1)}, f32[512,512]{1,0:T(8,128)}, u32[]{:S(2)}) copy-start(f32[512,512]{1,0:T(8,128)} %get-tuple-element.134) | copy-start | bytes 3145732 | tf_op jit(solution)/shard_map/while
  241.0 13.7 %collective-permute-start = (f32[1280,128]{1,0:T(8,128)S(1)}, f32[1280,128]{1,0:T(8,128)S(1)}, u32[]{:S(2)}, u32[]{:S(2)}) collective-permute-start(f32[1280,128]{1,0:T(8,128)S(1)} %slice_dynamic-update-slice_fusion.35), channel_id=1, source_target_pairs={{64,0},{128,64},{192,128},{256,192},{320,256},{384,320},{448,384},... | collective-permute-start | bytes 1966088 | tf_op jit(solution)/shard_map/while/body/eval_jaxpr/ppermute | solution.py:126
  254.6 7.9 %copy-start.3 = (bf16[1,512,512]{2,1,0:T(8,128)(2,1)S(1)}, bf16[1,512,512]{2,1,0:T(8,128)(2,1)}, u32[]{:S(2)}) copy-start(bf16[1,512,512]{2,1,0:T(8,128)(2,1)} %param.12) | copy-start | bytes 1572868
  254.6 11.9 %collective-permute-start.4 = (f32[1280,128]{1,0:T(8,128)S(1)}, f32[1280,128]{1,0:T(8,128)}, u32[]{:S(2)}, u32[]{:S(2)}) collective-permute-start(f32[1280,128]{1,0:T(8,128)S(1)} %get-tuple-element.24), channel_id=1, source_target_pairs={{0,1},{2,3},{4,5},{6,7},{8,9},{10,11},{12,13},{14,15},{16,17},{18,... | collective-permute-start | bytes 1966088 | tf_op jit(solution)/shard_map/ppermute | solution.py:131
  267.4 2.4 copy-start.4

commit v5 on v4

--- a/solution.py
+++ b/solution.py
@@ -55,19 +55,23 @@
 
 def unpack(packed, width):
     size = width // BLOCKS
+    zero = jnp.zeros((size, size), packed.dtype)
     blocks = {}
     k = 0
     for i in range(BLOCKS):
         for j in range(i + 1):
             blocks[i, j] = packed[k * size : (k + 1) * size]
             k += 1
-    rows = [
-        jnp.concatenate(
-            [blocks[i, j] if i >= j else blocks[j, i].T for j in range(BLOCKS)], axis=1
-        )
-        for i in range(BLOCKS)
-    ]
-    return jnp.concatenate(rows, axis=0)
+    lower = jnp.concatenate(
+        [
+            jnp.concatenate([blocks[i, j] if i >= j else zero for j in range(BLOCKS)], axis=1)
+            for i in range(BLOCKS)
+        ],
+        axis=0,
+    )
+    rows = lax.broadcasted_iota(jnp.int32, lower.shape, 0) // size
+    cols = lax.broadcasted_iota(jnp.int32, lower.shape, 1) // size
+    return jnp.where(rows >= cols, lower, lower.T)
 
 
 def symmetrize(matrix):
@@ -125,8 +129,8 @@
         )
         return lax.ppermute(pack(advanced), ("col", "core"), down)
 
-    first = lax.ppermute(pack(chain_own), ("col", "core"), down)
-    packed = lax.fori_loop(0, groups - 2, sweep, first)
+    start = jnp.zeros((BLOCKS * (BLOCKS + 1) // 2 * width // BLOCKS, width // BLOCKS), jnp.float32)
+    packed = lax.fori_loop(0, groups - 1, sweep, start)
     own_map = jnp.where(core == 0, chain_own, own_of(other))
     shared = lax.ppermute(packed, "core", [(0, 1)])
     incoming = unpack(jnp.where(core == 0, packed, shared), width)

time: 275 us -> 266 us (0.967)
  local copies, waits for them, and re-layouts: 46.5 us -> 22.3 us
  matrix products: 42.2 us -> 55.4 us
    slice x25 -> x8, local copies, waits for them, and re-layouts: 17.9 us -> 0.36 us  [unpack(): blocks[i, j] = packed[k * size:(k + 1) * size]]
    ppermute x6 -> x7, waiting for transfers between devices: 70.5 us -> 82.7 us  [sweep(): return lax.ppermute(pack(advanced), ('col', 'core'), down)]
    transpose x6 -> x0, local copies, waits for them, and re-layouts: 10.7 us -> none  [unpack(): blocks[j, i]]
    dot_general x6 -> x7, matrix products: 13.7 us -> 23.8 us  [sweep(): jnp.dot(incoming, link_wide, precision=chain)]
    ppermute x1 -> x0, waiting for transfers between devices: 9.35 us -> none  [on_device(): first = lax.ppermute(pack(chain_own), ('col', 'core'), down)]
    another operation x6 -> x16, local copies, waits for them, and re-layouts: 6.43 us -> 0.13 us
    concatenate x7 -> x8, local copies, waits for them, and re-layouts: 5.15 us -> 10.5 us  [unpack(): jnp.concatenate([jnp.concatenate([blocks[i, j] if i >= j else zero for j...]
    while x60 -> x168, local copies, waits for them, and re-layouts: 0.6 us -> 5.56 us
where the time goes in v5:
time: 266 us; the launch traced here: 265 us
  waiting for transfers between devices  85.6 us (32%)
  blocking collectives  64.5 us (24%)
  matrix products  55.4 us (21%)
  local copies, waits for them, and re-layouts  22.3 us (8%)
  starting transfers between devices  19.5 us (7%)
  other arithmetic  14.7 us (6%)
    ppermute x7, waiting for transfers between devices, sweep(): return lax.ppermute(pack(advanced), ('col', 'core'), down)  82.7 us
    all_to_all x2, blocking collectives, scatter_sum(): return jnp.sum(lax.all_to_all(pieces, axis, 0, 0), axis=0)  36.8 us
    all_to_all x2, blocking collectives, gather_all(): gathered = lax.all_to_all(spread, axis, 0, 0)  27.7 us
    dot_general x7, matrix products, sweep(): jnp.dot(incoming, link_wide, precision=chain)  23.8 us
    ppermute x7, starting transfers between devices, sweep(): return lax.ppermute(pack(advanced), ('col', 'core'), down)  13.4 us
    concatenate x8, local copies, waits for them, and re-layouts, unpack(): jnp.concatenate([jnp.concatenate([blocks[i, j] if i >= j else zero for j...  10.5 us
    dot_general x7, matrix products, sweep(): jnp.dot(link_wide.T, jnp.dot(incoming, link_wide, precision=chain), preci...  7.33 us
    while x168, local copies, waits for them, and re-layouts  5.56 us
  transfers between devices with their start and end apart: 10, of which 8 were waited for; matrix products, arithmetic and copies ran while one was open for 7% of the time, Pallas kernels for 0%

profile of v5, /device:TPU:192, one launch (start us, length us, event | category | flops | bytes accessed | tf_op | source)
XLA Modules:
  0.0 265.1 jit_solution(6737243828145647114)
XLA Ops:
  5.2 2.0 fusion.30
  7.2 2.7 %fusion.16 = f32[512,512]{1,0:T(8,128)S(1)} fusion(bf16[1,1,2,512,512]{4,3,2,1,0:T(8,128)(2,1)} %param.9, f32[2,512,512]{2,1,0:T(8,128)} %fusion.30, pred[2]{0:T(512)(128)(4,1)S(1)} %get-tuple-element.106), kind=kOutput, calls=%fused_computation.41 | convolution fusion | flops 538181632 | bytes 4194306 | tf_op jit(solution)/shard_map/sij,sik->jk/dot_general | solution.py:105
  14.2 3.0 %collective-permute-done.1 = f32[512,512]{1,0:T(8,128)} collective-permute-done((f32[512,512]{1,0:T(8,128)}, f32[512,512]{1,0:T(8,128)}, u32[]{:S(2)}, u32[]{:S(2)}) %collective-permute-start.1) | collective-permute-done | bytes 1048608 | tf_op jit(solution)/shard_map/ppermute | solution.py:12
  17.2 1.9 fusion.22
  19.1 19.2 %all_to_all.20 = f32[4,128,512]{2,1,0:T(8,128)S(1)} all-to-all(f32[4,128,512]{2,1,0:T(8,128)S(1)} %bitcast.91), channel_id=1, replica_groups=mesh['col'=8,'y'=8,'x'=4,'core'=2] {'x'}, dimensions={0} | all-to-all | bytes 2097152 | tf_op jit(solution)/shard_map/all_to_all | solution.py:18
  38.4 17.6 %all_to_all.21 = f32[8,16,512]{2,1,0:T(8,128)S(1)} all-to-all(f32[8,16,512]{2,1,0:T(8,128)S(1)} %bitcast.92), channel_id=1, replica_groups=mesh['col'=8,'y'=8,'x'=4,'core'=2] {'y'}, dimensions={0} | all-to-all | bytes 524288 | tf_op jit(solution)/shard_map/all_to_all | solution.py:18
  56.0 13.0 %all_to_all.22 = f32[8,16,512]{2,1,0:T(8,128)S(1)} all-to-all(f32[8,16,512]{2,1,0:T(8,128)S(1)} %broadcast_in_dim.45), channel_id=1, replica_groups=mesh['col'=8,'y'=8,'x'=4,'core'=2] {'y'}, dimensions={0} | all-to-all | bytes 524288 | tf_op jit(solution)/shard_map/all_to_all | solution.py:24
  69.2 14.7 %all_to_all.23 = f32[4,128,512]{2,1,0:T(8,128)} all-to-all(f32[4,128,512]{2,1,0:T(8,128)S(1)} %broadcast_in_dim.47), channel_id=1, replica_groups=mesh['col'=8,'y'=8,'x'=4,'core'=2] {'x'}, dimensions={0} | all-to-all | bytes 2097152 | tf_op jit(solution)/shard_map/all_to_all | solution.py:24
  86.9 2.0 fusion.35
  90.2 1.9 fusion.27
  95.7 148.3 %while.13 = (s32[]{:T(128)}, f32[1280,128]{1,0:T(8,128)S(1)}, f32[512,512]{1,0:T(8,128)S(1)}, f32[512,512]{1,0:T(8,128)}, s32[]{:T(128)}, /*index=5*/f32[]{:T(128)}) while((s32[]{:T(128)}, f32[1280,128]{1,0:T(8,128)S(1)}, f32[512,512]{1,0:T(8,128)S(1)}, f32[512,512]{1,0:T(8,128)}, s32[]{:T(128)}, /*index=5*/f32[]{:T(128)}) %tuple.59), condition=%wide.region_4.5_spmd, body=%wide.region_3.4_spmd.sunk | while | flops 1618742784 | bytes 23668052 | solution.py:133
  98.5 3.4 %fusion.85 = f32[512,512]{1,0:T(8,128)S(1)} fusion(f32[512,512]{1,0:T(8,128)S(1)} %get-tuple-element.172, f32[512,512]{0,1:T(8,128)} %copy.21, s32[512]{0:T(512)S(1)} %get-tuple-element.156, s32[512]{0:T(512)S(1)} %get-tuple-element.157, pred[512]{0:T(512)(128)(4,1)} %fusion.84, f32[128,128]{1,0:T(8,128)} %copy-done.10, ...), kind=kOutput, calls=%fused_computation.7.clone.1 | convolution fusion | flops 809762816 | bytes 4002304 | tf_op jit(solution)/shard_map/while/body/eval_jaxpr/dot_general | solution.py:128
  103.2 1.9 collective-permute-start
  105.1 12.1 %collective-permute-done = f32[1280,128]{1,0:T(8,128)S(1)} collective-permute-done((f32[1280,128]{1,0:T(8,128)S(1)}, f32[1280,128]{1,0:T(8,128)S(1)}, u32[]{:S(2)}, u32[]{:S(2)}) %collective-permute-start) | collective-permute-done | bytes 655392 | tf_op jit(solution)/shard_map/while/body/eval_jaxpr/ppermute | solution.py:130
  120.0 3.4 %fusion.85 = f32[512,512]{1,0:T(8,128)S(1)} fusion(f32[512,512]{1,0:T(8,128)S(1)} %get-tuple-element.172, f32[512,512]{0,1:T(8,128)} %copy.21, s32[512]{0:T(512)S(1)} %get-tuple-element.156, s32[512]{0:T(512)S(1)} %get-tuple-element.157, pred[512]{0:T(512)(128)(4,1)} %fusion.84, f32[128,128]{1,0:T(8,128)} %copy-done.10, ...), kind=kOutput, calls=%fused_computation.7.clone.1 | convolution fusion | flops 809762816 | bytes 4002304 | tf_op jit(solution)/shard_map/while/body/eval_jaxpr/dot_general | solution.py:128
  126.6 11.8 %collective-permute-done = f32[1280,128]{1,0:T(8,128)S(1)} collective-permute-done((f32[1280,128]{1,0:T(8,128)S(1)}, f32[1280,128]{1,0:T(8,128)S(1)}, u32[]{:S(2)}, u32[]{:S(2)}) %collective-permute-start) | collective-permute-done | bytes 655392 | tf_op jit(solution)/shard_map/while/body/eval_jaxpr/ppermute | solution.py:130
  141.2 3.4 %fusion.85 = f32[512,512]{1,0:T(8,128)S(1)} fusion(f32[512,512]{1,0:T(8,128)S(1)} %get-tuple-element.172, f32[512,512]{0,1:T(8,128)} %copy.21, s32[512]{0:T(512)S(1)} %get-tuple-element.156, s32[512]{0:T(512)S(1)} %get-tuple-element.157, pred[512]{0:T(512)(128)(4,1)} %fusion.84, f32[128,128]{1,0:T(8,128)} %copy-done.10, ...), kind=kOutput, calls=%fused_computation.7.clone.1 | convolution fusion | flops 809762816 | bytes 4002304 | tf_op jit(solution)/shard_map/while/body/eval_jaxpr/dot_general | solution.py:128
  145.8 1.9 collective-permute-start
  147.7 11.8 %collective-permute-done = f32[1280,128]{1,0:T(8,128)S(1)} collective-permute-done((f32[1280,128]{1,0:T(8,128)S(1)}, f32[1280,128]{1,0:T(8,128)S(1)}, u32[]{:S(2)}, u32[]{:S(2)}) %collective-permute-start) | collective-permute-done | bytes 655392 | tf_op jit(solution)/shard_map/while/body/eval_jaxpr/ppermute | solution.py:130
  162.3 3.4 %fusion.85 = f32[512,512]{1,0:T(8,128)S(1)} fusion(f32[512,512]{1,0:T(8,128)S(1)} %get-tuple-element.172, f32[512,512]{0,1:T(8,128)} %copy.21, s32[512]{0:T(512)S(1)} %get-tuple-element.156, s32[512]{0:T(512)S(1)} %get-tuple-element.157, pred[512]{0:T(512)(128)(4,1)} %fusion.84, f32[128,128]{1,0:T(8,128)} %copy-done.10, ...), kind=kOutput, calls=%fused_computation.7.clone.1 | convolution fusion | flops 809762816 | bytes 4002304 | tf_op jit(solution)/shard_map/while/body/eval_jaxpr/dot_general | solution.py:128
  168.9 11.8 %collective-permute-done = f32[1280,128]{1,0:T(8,128)S(1)} collective-permute-done((f32[1280,128]{1,0:T(8,128)S(1)}, f32[1280,128]{1,0:T(8,128)S(1)}, u32[]{:S(2)}, u32[]{:S(2)}) %collective-permute-start) | collective-permute-done | bytes 655392 | tf_op jit(solution)/shard_map/while/body/eval_jaxpr/ppermute | solution.py:130
  183.4 3.4 %fusion.85 = f32[512,512]{1,0:T(8,128)S(1)} fusion(f32[512,512]{1,0:T(8,128)S(1)} %get-tuple-element.172, f32[512,512]{0,1:T(8,128)} %copy.21, s32[512]{0:T(512)S(1)} %get-tuple-element.156, s32[512]{0:T(512)S(1)} %get-tuple-element.157, pred[512]{0:T(512)(128)(4,1)} %fusion.84, f32[128,128]{1,0:T(8,128)} %copy-done.10, ...), kind=kOutput, calls=%fused_computation.7.clone.1 | convolution fusion | flops 809762816 | bytes 4002304 | tf_op jit(solution)/shard_map/while/body/eval_jaxpr/dot_general | solution.py:128
  190.0 11.8 %collective-permute-done = f32[1280,128]{1,0:T(8,128)S(1)} collective-permute-done((f32[1280,128]{1,0:T(8,128)S(1)}, f32[1280,128]{1,0:T(8,128)S(1)}, u32[]{:S(2)}, u32[]{:S(2)}) %collective-permute-start) | collective-permute-done | bytes 655392 | tf_op jit(solution)/shard_map/while/body/eval_jaxpr/ppermute | solution.py:130
  204.5 3.4 %fusion.85 = f32[512,512]{1,0:T(8,128)S(1)} fusion(f32[512,512]{1,0:T(8,128)S(1)} %get-tuple-element.172, f32[512,512]{0,1:T(8,128)} %copy.21, s32[512]{0:T(512)S(1)} %get-tuple-element.156, s32[512]{0:T(512)S(1)} %get-tuple-element.157, pred[512]{0:T(512)(128)(4,1)} %fusion.84, f32[128,128]{1,0:T(8,128)} %copy-done.10, ...), kind=kOutput, calls=%fused_computation.7.clone.1 | convolution fusion | flops 809762816 | bytes 4002304 | tf_op jit(solution)/shard_map/while/body/eval_jaxpr/dot_general | solution.py:128
  211.1 11.8 %collective-permute-done = f32[1280,128]{1,0:T(8,128)S(1)} collective-permute-done((f32[1280,128]{1,0:T(8,128)S(1)}, f32[1280,128]{1,0:T(8,128)S(1)}, u32[]{:S(2)}, u32[]{:S(2)}) %collective-permute-start) | collective-permute-done | bytes 655392 | tf_op jit(solution)/shard_map/while/body/eval_jaxpr/ppermute | solution.py:130
  225.7 3.4 %fusion.85 = f32[512,512]{1,0:T(8,128)S(1)} fusion(f32[512,512]{1,0:T(8,128)S(1)} %get-tuple-element.172, f32[512,512]{0,1:T(8,128)} %copy.21, s32[512]{0:T(512)S(1)} %get-tuple-element.156, s32[512]{0:T(512)S(1)} %get-tuple-element.157, pred[512]{0:T(512)(128)(4,1)} %fusion.84, f32[128,128]{1,0:T(8,128)} %copy-done.10, ...), kind=kOutput, calls=%fused_computation.7.clone.1 | convolution fusion | flops 809762816 | bytes 4002304 | tf_op jit(solution)/shard_map/while/body/eval_jaxpr/dot_general | solution.py:128
  232.3 11.8 %collective-permute-done = f32[1280,128]{1,0:T(8,128)S(1)} collective-permute-done((f32[1280,128]{1,0:T(8,128)S(1)}, f32[1280,128]{1,0:T(8,128)S(1)}, u32[]{:S(2)}, u32[]{:S(2)}) %collective-permute-start) | collective-permute-done | bytes 655392 | tf_op jit(solution)/shard_map/while/body/eval_jaxpr/ppermute | solution.py:130
  244.0 2.3 collective-permute-start.3
  246.3 3.1 %fusion.33 = f32[512,512]{1,0:T(8,128)} fusion(f32[512,512]{1,0:T(8,128)} %collective-permute-done.2, bf16[1,512,512]{2,1,0:T(8,128)(2,1)} %param.11), kind=kOutput, calls=%fused_computation.68 | convolution fusion | flops 805306368 | bytes 2621440 | tf_op jit(solution)/shard_map/dot_general | solution.py:117
  249.4 2.5 copy.18
  251.9 2.3 fusion.25
  258.2 3.5 %broadcast_multiply_fusion = (f32[512,512]{1,0:T(8,128)S(1)}, f32[512,512]{1,0:T(8,128)S(1)}) fusion(f32[512,512]{1,0:T(8,128)S(1)} %get-tuple-element.176, f32[512,512]{0,1:T(8,128)} %copy.17, s32[512]{0:T(512)S(1)} %copy-done.22, s32[512]{0:T(512)S(1)} %copy-done.23, pred[512]{0:T(512)(128)(4,1)} %fusion.56, f32[128,128]{1,0:T(8,128)S(1)} %get-tuple-element.94, ...), kind=kOutput, calls=%fused_computation.79 | convolution fusion | flops 810024960 | bytes 5050880 | tf_op jit(solution)/shard_map/dot_general | solution.py:137
  (296 shorter events, 60.1 us)
Async XLA Ops:
  0.6 4.5 %copy-start = (bf16[1,1,2,512,512]{4,3,2,1,0:T(8,128)(2,1)S(1)}, bf16[1,1,2,512,512]{4,3,2,1,0:T(8,128)(2,1)}, u32[]{:S(2)}) copy-start(bf16[1,1,2,512,512]{4,3,2,1,0:T(8,128)(2,1)} %param.10) | copy-start | bytes 3145732
  0.6 4.5 %copy-start.2 = (bf16[1,512,512]{2,1,0:T(8,128)(2,1)S(1)}, bf16[1,512,512]{2,1,0:T(8,128)(2,1)}, u32[]{:S(2)}) copy-start(bf16[1,512,512]{2,1,0:T(8,128)(2,1)} %param.12) | copy-start | bytes 1572868
  7.2 2.7 %copy-start.21 = (f32[1,8,512]{2,1,0:T(8,128)S(1)}, f32[1,8,512]{2,1,0:T(8,128)}, u32[]{:S(2)}) copy-start(f32[1,8,512]{2,1,0:T(8,128)} %param.13) | copy-start | bytes 49156
  9.9 1.0 copy-start.12
  12.3 4.9 %collective-permute-start.1 = (f32[512,512]{1,0:T(8,128)}, f32[512,512]{1,0:T(8,128)}, u32[]{:S(2)}, u32[]{:S(2)}) collective-permute-start(f32[512,512]{1,0:T(8,128)} %fusion.20), channel_id=1, source_target_pairs={{0,1},{1,0},{2,3},{3,2},{4,5},{5,4},{6,7},{7,6},{8,9},{9,8},{10,11... | collective-permute-start | bytes 3145736 | tf_op jit(solution)/shard_map/ppermute | solution.py:12
  56.0 30.9 %copy-start.13 = (bf16[1,512,512]{2,1,0:T(8,128)(2,1)S(1)}, bf16[1,512,512]{2,1,0:T(8,128)(2,1)}, u32[]{:S(2)}) copy-start(bf16[1,512,512]{2,1,0:T(8,128)(2,1)} %param.11) | copy-start | bytes 1572868
  83.9 10.0 %collective-permute-start.2 = (f32[512,512]{1,0:T(8,128)}, f32[512,512]{1,0:T(8,128)}, u32[]{:S(2)}, u32[]{:S(2)}) collective-permute-start(f32[512,512]{1,0:T(8,128)} %bitcast.13), channel_id=1, source_target_pairs={{0,1},{1,0},{2,3},{3,2},{4,5},{5,4},{6,7},{7,6},{8,9},{9,8},{10,11... | collective-permute-start | bytes 3145736 | tf_op jit(solution)/shard_map/ppermute | solution.py:12
  96.4 0.7 copy-start.10
  98.5 3.4 %copy-start.1 = (f32[512,512]{1,0:T(8,128)S(1)}, f32[512,512]{1,0:T(8,128)}, u32[]{:S(2)}) copy-start(f32[512,512]{1,0:T(8,128)} %get-tuple-element.173) | copy-start | bytes 3145732 | tf_op jit(solution)/shard_map/while
  103.2 14.0 %collective-permute-start = (f32[1280,128]{1,0:T(8,128)S(1)}, f32[1280,128]{1,0:T(8,128)S(1)}, u32[]{:S(2)}, u32[]{:S(2)}) collective-permute-start(f32[1280,128]{1,0:T(8,128)S(1)} %slice_dynamic-update-slice_fusion.26), channel_id=1, source_target_pairs={{64,0},{128,64},{192,128},{256,192},{320,256},{384,320},{448,384},... | collective-permute-start | bytes 1966088 | tf_op jit(solution)/shard_map/while/body/eval_jaxpr/ppermute | solution.py:130
  117.9 0.7 copy-start.10
  120.0 3.4 %copy-start.1 = (f32[512,512]{1,0:T(8,128)S(1)}, f32[512,512]{1,0:T(8,128)}, u32[]{:S(2)}) copy-start(f32[512,512]{1,0:T(8,128)} %get-tuple-element.173) | copy-start | bytes 3145732 | tf_op jit(solution)/shard_map/while
  124.7 13.7 %collective-permute-start = (f32[1280,128]{1,0:T(8,128)S(1)}, f32[1280,128]{1,0:T(8,128)S(1)}, u32[]{:S(2)}, u32[]{:S(2)}) collective-permute-start(f32[1280,128]{1,0:T(8,128)S(1)} %slice_dynamic-update-slice_fusion.26), channel_id=1, source_target_pairs={{64,0},{128,64},{192,128},{256,192},{320,256},{384,320},{448,384},... | collective-permute-start | bytes 1966088 | tf_op jit(solution)/shard_map/while/body/eval_jaxpr/ppermute | solution.py:130
  139.0 0.7 copy-start.10
  141.1 3.4 %copy-start.1 = (f32[512,512]{1,0:T(8,128)S(1)}, f32[512,512]{1,0:T(8,128)}, u32[]{:S(2)}) copy-start(f32[512,512]{1,0:T(8,128)} %get-tuple-element.173) | copy-start | bytes 3145732 | tf_op jit(solution)/shard_map/while
  145.8 13.7 %collective-permute-start = (f32[1280,128]{1,0:T(8,128)S(1)}, f32[1280,128]{1,0:T(8,128)S(1)}, u32[]{:S(2)}, u32[]{:S(2)}) collective-permute-start(f32[1280,128]{1,0:T(8,128)S(1)} %slice_dynamic-update-slice_fusion.26), channel_id=1, source_target_pairs={{64,0},{128,64},{192,128},{256,192},{320,256},{384,320},{448,384},... | collective-permute-start | bytes 1966088 | tf_op jit(solution)/shard_map/while/body/eval_jaxpr/ppermute | solution.py:130
  160.1 0.7 copy-start.10
  162.3 3.4 %copy-start.1 = (f32[512,512]{1,0:T(8,128)S(1)}, f32[512,512]{1,0:T(8,128)}, u32[]{:S(2)}) copy-start(f32[512,512]{1,0:T(8,128)} %get-tuple-element.173) | copy-start | bytes 3145732 | tf_op jit(solution)/shard_map/while
  166.9 13.7 %collective-permute-start = (f32[1280,128]{1,0:T(8,128)S(1)}, f32[1280,128]{1,0:T(8,128)S(1)}, u32[]{:S(2)}, u32[]{:S(2)}) collective-permute-start(f32[1280,128]{1,0:T(8,128)S(1)} %slice_dynamic-update-slice_fusion.26), channel_id=1, source_target_pairs={{64,0},{128,64},{192,128},{256,192},{320,256},{384,320},{448,384},... | collective-permute-start | bytes 1966088 | tf_op jit(solution)/shard_map/while/body/eval_jaxpr/ppermute | solution.py:130
  181.3 0.7 copy-start.10
  183.4 3.4 %copy-start.1 = (f32[512,512]{1,0:T(8,128)S(1)}, f32[512,512]{1,0:T(8,128)}, u32[]{:S(2)}) copy-start(f32[512,512]{1,0:T(8,128)} %get-tuple-element.173) | copy-start | bytes 3145732 | tf_op jit(solution)/shard_map/while
  188.1 13.7 %collective-permute-start = (f32[1280,128]{1,0:T(8,128)S(1)}, f32[1280,128]{1,0:T(8,128)S(1)}, u32[]{:S(2)}, u32[]{:S(2)}) collective-permute-start(f32[1280,128]{1,0:T(8,128)S(1)} %slice_dynamic-update-slice_fusion.26), channel_id=1, source_target_pairs={{64,0},{128,64},{192,128},{256,192},{320,256},{384,320},{448,384},... | collective-permute-start | bytes 1966088 | tf_op jit(solution)/shard_map/while/body/eval_jaxpr/ppermute | solution.py:130
  204.5 3.4 %copy-start.1 = (f32[512,512]{1,0:T(8,128)S(1)}, f32[512,512]{1,0:T(8,128)}, u32[]{:S(2)}) copy-start(f32[512,512]{1,0:T(8,128)} %get-tuple-element.173) | copy-start | bytes 3145732 | tf_op jit(solution)/shard_map/while
  209.2 13.7 %collective-permute-start = (f32[1280,128]{1,0:T(8,128)S(1)}, f32[1280,128]{1,0:T(8,128)S(1)}, u32[]{:S(2)}, u32[]{:S(2)}) collective-permute-start(f32[1280,128]{1,0:T(8,128)S(1)} %slice_dynamic-update-slice_fusion.26), channel_id=1, source_target_pairs={{64,0},{128,64},{192,128},{256,192},{320,256},{384,320},{448,384},... | collective-permute-start | bytes 1966088 | tf_op jit(solution)/shard_map/while/body/eval_jaxpr/ppermute | solution.py:130
  225.7 3.4 %copy-start.1 = (f32[512,512]{1,0:T(8,128)S(1)}, f32[512,512]{1,0:T(8,128)}, u32[]{:S(2)}) copy-start(f32[512,512]{1,0:T(8,128)} %get-tuple-element.173) | copy-start | bytes 3145732 | tf_op jit(solution)/shard_map/while
  230.3 13.7 %collective-permute-start = (f32[1280,128]{1,0:T(8,128)S(1)}, f32[1280,128]{1,0:T(8,128)S(1)}, u32[]{:S(2)}, u32[]{:S(2)}) collective-permute-start(f32[1280,128]{1,0:T(8,128)S(1)} %slice_dynamic-update-slice_fusion.26), channel_id=1, source_target_pairs={{64,0},{128,64},{192,128},{256,192},{320,256},{384,320},{448,384},... | collective-permute-start | bytes 1966088 | tf_op jit(solution)/shard_map/while/body/eval_jaxpr/ppermute | solution.py:130
  244.0 7.9 %copy-start.3 = (bf16[1,512,512]{2,1,0:T(8,128)(2,1)S(1)}, bf16[1,512,512]{2,1,0:T(8,128)(2,1)}, u32[]{:S(2)}) copy-start(bf16[1,512,512]{2,1,0:T(8,128)(2,1)} %param.12) | copy-start | bytes 1572868
  244.0 11.9 %collective-permute-start.3 = (f32[1280,128]{1,0:T(8,128)S(1)}, f32[1280,128]{1,0:T(8,128)}, u32[]{:S(2)}, u32[]{:S(2)}) collective-permute-start(f32[1280,128]{1,0:T(8,128)S(1)} %get-tuple-element.72), channel_id=1, source_target_pairs={{0,1},{2,3},{4,5},{6,7},{8,9},{10,11},{12,13},{14,15},{16,17},{18,... | collective-permute-start | bytes 1966088 | tf_op jit(solution)/shard_map/ppermute | solution.py:135
  256.1 0.7 copy-start.19
  256.1 2.1 copy-start.22
  256.1 2.1 copy-start.23
  258.2 3.5 %copy-start.4 = (f32[2,512,512]{2,1,0:T(8,128)S(1)}, f32[2,512,512]{2,1,0:T(8,128)}, u32[]{:S(2)}) copy-start(f32[2,512,512]{2,1,0:T(8,128)} %fusion.30) | copy-start | bytes 6291460
  (50 other events, 33.6 us)

commit v6 on v4

--- a/solution.py
+++ b/solution.py
@@ -125,9 +125,9 @@
         )
         return lax.ppermute(pack(advanced), ("col", "core"), down)
 
-    first = lax.ppermute(pack(chain_own), ("col", "core"), down)
-    packed = lax.fori_loop(0, groups - 2, sweep, first)
-    own_map = jnp.where(core == 0, chain_own, own_of(other))
+    start = jnp.zeros((BLOCKS * (BLOCKS + 1) // 2 * width // BLOCKS, width // BLOCKS), jnp.float32)
+    packed = lax.fori_loop(0, groups - 1, sweep, start)
+    own_map = jnp.where(core == 0, chain_own, lax.ppermute(chain_own, "core", [(0, 1)]))
     shared = lax.ppermute(packed, "core", [(0, 1)])
     incoming = unpack(jnp.where(core == 0, packed, shared), width)
     product = jnp.dot(incoming, link_wide, precision=chain)

time: 275 us -> 236 us (0.86)
  the two profiles are of different devices: /device:TPU:192 before, /device:TPU:1 now
where the time goes in v6:
time: 236 us; the launch traced here: 234 us
  waiting for transfers between devices  91.4 us (39%)
  blocking collectives  55.4 us (23%)
  matrix products  37 us (16%)
  starting transfers between devices  22.8 us (10%)
  local copies, waits for them, and re-layouts  18.3 us (8%)
  other arithmetic  5.57 us (2%)
    ppermute x1, waiting for transfers between devices, on_device(): shared = lax.ppermute(packed, 'core', [(0, 1)])  88.8 us
    all_to_all x2, blocking collectives, scatter_sum(): return jnp.sum(lax.all_to_all(pieces, axis, 0, 0), axis=0)  29.4 us
    all_to_all x2, blocking collectives, gather_all(): gathered = lax.all_to_all(spread, axis, 0, 0)  26 us
    ppermute x2, starting transfers between devices, swap_cores(): return lax.ppermute(value, 'core', [(0, 1), (1, 0)])  15.3 us
    dot_general x7, matrix products, sweep(): jnp.dot(incoming, link_wide, precision=chain)  14.9 us
    dot_general x7, matrix products, sweep(): jnp.dot(link_wide.T, jnp.dot(incoming, link_wide, precision=chain), preci...  7.33 us
    slice x29, local copies, waits for them, and re-layouts, unpack(): blocks[i, j] = packed[k * size:(k + 1) * size]  7.03 us
    ppermute x7, starting transfers between devices, sweep(): return lax.ppermute(pack(advanced), ('col', 'core'), down)  4.92 us
  transfers between devices with their start and end apart: 11, of which 2 were waited for; matrix products, arithmetic and copies ran while one was open for 4% of the time, Pallas kernels for 0%

profile of v6, /device:TPU:1, one launch (start us, length us, event | category | flops | bytes accessed | tf_op | source)
XLA Modules:
  0.0 233.5 jit_solution(3645678882852269305)
XLA Ops:
  1.9 3.2 %fusion.64 = f32[2,512,512]{2,1,0:T(8,128)} fusion(bf16[1,1,2,512,512]{4,3,2,1,0:T(8,128)(2,1)S(1)} %copy-done, bf16[1,512,512]{2,1,0:T(8,128)(2,1)} %param.12), kind=kOutput, calls=%fused_computation.90 | convolution fusion | flops 536870912 | bytes 3670016 | tf_op jit(solution)/shard_map/sij,jk->sik/dot_general | solution.py:97
  5.9 2.7 %fusion.29 = f32[512,512]{1,0:T(8,128)S(1)} fusion(bf16[1,1,2,512,512]{4,3,2,1,0:T(8,128)(2,1)} %param.9, f32[2,512,512]{2,1,0:T(8,128)} %fusion.64, pred[2]{0:T(512)(128)(4,1)S(1)} %get-tuple-element.64), kind=kOutput, calls=%fused_computation.53 | convolution fusion | flops 538181632 | bytes 4194306 | tf_op jit(solution)/shard_map/sij,sik->jk/dot_general | solution.py:101
  8.6 1.4 fusion.32
  10.0 8.7 %collective-permute-start.1 = (f32[512,512]{1,0:T(8,128)}, f32[512,512]{1,0:T(8,128)}, u32[]{:S(2)}, u32[]{:S(2)}) collective-permute-start(f32[512,512]{1,0:T(8,128)} %fusion.32), channel_id=1, source_target_pairs={{0,1},{1,0},{2,3},{3,2},{4,5},{5,4},{6,7},{7,6},{8,9},{9,8},{10,11... | collective-permute-start | bytes 3145736 | tf_op jit(solution)/shard_map/ppermute | solution.py:12
  18.8 2.6 %collective-permute-done.1 = f32[512,512]{1,0:T(8,128)} collective-permute-done((f32[512,512]{1,0:T(8,128)}, f32[512,512]{1,0:T(8,128)}, u32[]{:S(2)}, u32[]{:S(2)}) %collective-permute-start.1) | collective-permute-done | bytes 1048608 | tf_op jit(solution)/shard_map/ppermute | solution.py:12
  21.4 1.7 fusion.34
  23.0 17.2 %all_to_all.20 = f32[4,128,512]{2,1,0:T(8,128)S(1)} all-to-all(f32[4,128,512]{2,1,0:T(8,128)S(1)} %bitcast.92), channel_id=1, replica_groups=mesh['col'=8,'y'=8,'x'=4,'core'=2] {'x'}, dimensions={0} | all-to-all | bytes 2097152 | tf_op jit(solution)/shard_map/all_to_all | solution.py:18
  40.4 12.1 %all_to_all.21 = f32[8,16,512]{2,1,0:T(8,128)S(1)} all-to-all(f32[8,16,512]{2,1,0:T(8,128)S(1)} %bitcast.93), channel_id=1, replica_groups=mesh['col'=8,'y'=8,'x'=4,'core'=2] {'y'}, dimensions={0} | all-to-all | bytes 524288 | tf_op jit(solution)/shard_map/all_to_all | solution.py:18
  52.5 12.2 %all_to_all.22 = f32[8,16,512]{2,1,0:T(8,128)S(1)} all-to-all(f32[8,16,512]{2,1,0:T(8,128)S(1)} %broadcast_in_dim.45), channel_id=1, replica_groups=mesh['col'=8,'y'=8,'x'=4,'core'=2] {'y'}, dimensions={0} | all-to-all | bytes 524288 | tf_op jit(solution)/shard_map/all_to_all | solution.py:24
  64.9 13.8 %all_to_all.23 = f32[4,128,512]{2,1,0:T(8,128)S(1)} all-to-all(f32[4,128,512]{2,1,0:T(8,128)S(1)} %broadcast_in_dim.47), channel_id=1, replica_groups=mesh['col'=8,'y'=8,'x'=4,'core'=2] {'x'}, dimensions={0} | all-to-all | bytes 2097152 | tf_op jit(solution)/shard_map/all_to_all | solution.py:24
  78.7 6.5 %collective-permute-start.2 = (f32[512,512]{1,0:T(8,128)S(1)}, f32[512,512]{1,0:T(8,128)}, u32[]{:S(2)}, u32[]{:S(2)}) collective-permute-start(f32[512,512]{1,0:T(8,128)S(1)} %bitcast.90), channel_id=1, source_target_pairs={{0,1},{1,0},{2,3},{3,2},{4,5},{5,4},{6,7},{7,6},{8,9},{9,8},{10,11... | collective-permute-start | bytes 3145736 | tf_op jit(solution)/shard_map/ppermute | solution.py:12
  85.2 1.8 fusion.67
  87.0 1.3 copy.39
  88.4 2.1 fusion.61
  90.5 1.8 fusion.28
  92.5 43.7 %while.10 = (s32[]{:T(128)}, f32[1280,128]{1,0:T(8,128)S(1)}, f32[512,512]{1,0:T(8,128)S(1)}, f32[512,512]{1,0:T(8,128)}, s32[]{:T(128)}) while((s32[]{:T(128)}, f32[1280,128]{1,0:T(8,128)S(1)}, f32[512,512]{1,0:T(8,128)S(1)}, f32[512,512]{1,0:T(8,128)}, s32[]{:T(128)}) %tuple.53), condition=%wide.region_4.5_spmd, body=%wide.region_3.4_spmd.sunk | while | flops 1614217216 | bytes 19923072 | solution.py:129
  94.7 2.1 fusion.107
  100.9 2.1 fusion.107
  103.1 1.0 fusion.108
  107.2 2.1 fusion.107
  109.3 1.1 fusion.108
  113.4 2.1 fusion.107
  119.6 2.1 fusion.107
  121.8 1.0 fusion.108
  125.9 2.1 fusion.107
  132.1 2.1 fusion.107
  134.3 1.0 fusion.108
  136.2 1.3 collective-permute-start.3
  137.5 1.3 collective-permute-start.4
  138.8 88.8 %collective-permute-done.3 = f32[1280,128]{1,0:T(8,128)S(1)} collective-permute-done((f32[1280,128]{1,0:T(8,128)S(1)}, f32[1280,128]{1,0:T(8,128)S(1)}, u32[]{:S(2)}, u32[]{:S(2)}) %collective-permute-start.3) | collective-permute-done | bytes 655392 | tf_op jit(solution)/shard_map/ppermute | solution.py:131
  230.1 1.6 fusion.31
  231.7 1.9 fusion.78
  (186 shorter events, 27.5 us)
Async XLA Ops:
  0.6 1.2 copy-start
  0.6 4.4 %copy-start.7 = (s32[1,1,2]{2,1,0:T(1,128)S(1)}, s32[1,1,2]{2,1,0:T(1,128)}, u32[]{:S(2)}) copy-start(s32[1,1,2]{2,1,0:T(1,128)} %param.15) | copy-start | bytes 28
  0.7 4.4 %copy-start.5 = (bf16[1,1,2,512,512]{4,3,2,1,0:T(8,128)(2,1)S(1)}, bf16[1,1,2,512,512]{4,3,2,1,0:T(8,128)(2,1)}, u32[]{:S(2)}) copy-start(bf16[1,1,2,512,512]{4,3,2,1,0:T(8,128)(2,1)} %param.9) | copy-start | bytes 3145732
  1.9 3.6 %copy-start.3 = (bf16[1,512,512]{2,1,0:T(8,128)(2,1)S(1)}, bf16[1,512,512]{2,1,0:T(8,128)(2,1)}, u32[]{:S(2)}) copy-start(bf16[1,512,512]{2,1,0:T(8,128)(2,1)} %param.12) | copy-start | bytes 1572868
  5.9 2.7 %copy-start.6 = (f32[1,8,512]{2,1,0:T(8,128)S(1)}, f32[1,8,512]{2,1,0:T(8,128)}, u32[]{:S(2)}) copy-start(f32[1,8,512]{2,1,0:T(8,128)} %param.13) | copy-start | bytes 49156
  10.0 11.4 %collective-permute-start.1 = (f32[512,512]{1,0:T(8,128)}, f32[512,512]{1,0:T(8,128)}, u32[]{:S(2)}, u32[]{:S(2)}) collective-permute-start(f32[512,512]{1,0:T(8,128)} %fusion.32), channel_id=1, source_target_pairs={{0,1},{1,0},{2,3},{3,2},{4,5},{5,4},{6,7},{7,6},{8,9},{9,8},{10,11... | collective-permute-start | bytes 3145736 | tf_op jit(solution)/shard_map/ppermute | solution.py:12
  78.7 13.6 %collective-permute-start.2 = (f32[512,512]{1,0:T(8,128)S(1)}, f32[512,512]{1,0:T(8,128)}, u32[]{:S(2)}, u32[]{:S(2)}) collective-permute-start(f32[512,512]{1,0:T(8,128)S(1)} %bitcast.90), channel_id=1, source_target_pairs={{0,1},{1,0},{2,3},{3,2},{4,5},{5,4},{6,7},{7,6},{8,9},{9,8},{10,11... | collective-permute-start | bytes 3145736 | tf_op jit(solution)/shard_map/ppermute | solution.py:12
  88.4 2.1 copy-start.4
  94.7 2.1 copy-start.1
  98.0 0.7 collective-permute-start
  100.9 2.1 copy-start.1
  104.3 0.7 collective-permute-start
  107.1 2.1 copy-start.1
  110.5 0.7 collective-permute-start
  113.4 2.1 copy-start.1
  116.8 0.7 collective-permute-start
  119.6 2.1 copy-start.1
  123.0 0.7 collective-permute-start
  125.9 2.1 copy-start.1
  129.3 0.7 collective-permute-start
  132.1 2.1 copy-start.1
  135.5 0.7 collective-permute-start
  136.2 91.4 %collective-permute-start.3 = (f32[1280,128]{1,0:T(8,128)S(1)}, f32[1280,128]{1,0:T(8,128)S(1)}, u32[]{:S(2)}, u32[]{:S(2)}) collective-permute-start(f32[1280,128]{1,0:T(8,128)S(1)} %get-tuple-element.24), channel_id=1, source_target_pairs={{0,1},{2,3},{4,5},{6,7},{8,9},{10,11},{12,13},{14,15},{16,17},{18,... | collective-permute-start | bytes 1966088 | tf_op jit(solution)/shard_map/ppermute | solution.py:131
  137.5 94.1 %collective-permute-start.4 = (f32[512,512]{1,0:T(8,128)}, f32[512,512]{1,0:T(8,128)}, u32[]{:S(2)}, u32[]{:S(2)}) collective-permute-start(f32[512,512]{1,0:T(8,128)} %get-tuple-element.140), channel_id=1, source_target_pairs={{0,1},{2,3},{4,5},{6,7},{8,9},{10,11},{12,13},{14,15},{16,17},{18,... | collective-permute-start | bytes 3145736 | tf_op jit(solution)/shard_map/ppermute | solution.py:130
  228.5 1.6 copy-start.2

commit v7 on v6

--- a/solution.py
+++ b/solution.py
@@ -31,9 +31,9 @@
     keep = lax.dynamic_slice_in_dim(value, core * half, half, 0)
     send = lax.dynamic_slice_in_dim(value, (1 - core) * half, half, 0)
     mine = keep + swap_cores(send)
+    for axis in CHIPS:
+        mine = scatter_sum(mine, axis)
     for axis in CHIPS[::-1]:
-        mine = scatter_sum(mine, axis)
-    for axis in CHIPS:
         mine = gather_all(mine, axis)
     return mine
 

time: 236 us -> 254 us (1.076)
  blocking collectives: 55.4 us -> 73 us
    all_to_all x2, blocking collectives: 29.4 us -> 38.8 us  [scatter_sum(): return jnp.sum(lax.all_to_all(pieces, axis, 0, 0), axis=0)]
    all_to_all x2, blocking collectives: 26 us -> 34.2 us  [gather_all(): gathered = lax.all_to_all(spread, axis, 0, 0)]
where the time goes in v7:
time: 254 us; the launch traced here: 252 us
  waiting for transfers between devices  91.6 us (36%)
  blocking collectives  73 us (29%)
  matrix products  37 us (15%)
  starting transfers between devices  23.2 us (9%)
  local copies, waits for them, and re-layouts  18.3 us (7%)
  other arithmetic  5.56 us (2%)
    ppermute x1, waiting for transfers between devices, on_device(): shared = lax.ppermute(packed, 'core', [(0, 1)])  89 us
    all_to_all x2, blocking collectives, scatter_sum(): return jnp.sum(lax.all_to_all(pieces, axis, 0, 0), axis=0)  38.8 us
    all_to_all x2, blocking collectives, gather_all(): gathered = lax.all_to_all(spread, axis, 0, 0)  34.2 us
    ppermute x2, starting transfers between devices, swap_cores(): return lax.ppermute(value, 'core', [(0, 1), (1, 0)])  15.7 us
    dot_general x7, matrix products, sweep(): jnp.dot(incoming, link_wide, precision=chain)  14.9 us
    dot_general x7, matrix products, sweep(): jnp.dot(link_wide.T, jnp.dot(incoming, link_wide, precision=chain), preci...  7.33 us
    slice x29, local copies, waits for them, and re-layouts, unpack(): blocks[i, j] = packed[k * size:(k + 1) * size]  7.03 us
  transfers between devices with their start and end apart: 11, of which 2 were waited for; matrix products, arithmetic and copies ran while one was open for 4% of the time, Pallas kernels for 0%

profile of v7, /device:TPU:1, one launch (start us, length us, event | category | flops | bytes accessed | tf_op | source)
XLA Modules:
  0.0 251.7 jit_solution(5344395342092436077)
XLA Ops:
  1.9 3.2 %fusion.64 = f32[2,512,512]{2,1,0:T(8,128)} fusion(bf16[1,1,2,512,512]{4,3,2,1,0:T(8,128)(2,1)S(1)} %copy-done, bf16[1,512,512]{2,1,0:T(8,128)(2,1)} %param.12), kind=kOutput, calls=%fused_computation.90 | convolution fusion | flops 536870912 | bytes 3670016 | tf_op jit(solution)/shard_map/sij,jk->sik/dot_general | solution.py:97
  5.9 2.7 %fusion.29 = f32[512,512]{1,0:T(8,128)S(1)} fusion(bf16[1,1,2,512,512]{4,3,2,1,0:T(8,128)(2,1)} %param.9, f32[2,512,512]{2,1,0:T(8,128)} %fusion.64, pred[2]{0:T(512)(128)(4,1)S(1)} %get-tuple-element.64), kind=kOutput, calls=%fused_computation.53 | convolution fusion | flops 538181632 | bytes 4194306 | tf_op jit(solution)/shard_map/sij,sik->jk/dot_general | solution.py:101
  8.6 1.4 fusion.32
  10.0 8.7 %collective-permute-start.1 = (f32[512,512]{1,0:T(8,128)}, f32[512,512]{1,0:T(8,128)}, u32[]{:S(2)}, u32[]{:S(2)}) collective-permute-start(f32[512,512]{1,0:T(8,128)} %fusion.32), channel_id=1, source_target_pairs={{0,1},{1,0},{2,3},{3,2},{4,5},{5,4},{6,7},{7,6},{8,9},{9,8},{10,11... | collective-permute-start | bytes 3145736 | tf_op jit(solution)/shard_map/ppermute | solution.py:12
  18.8 2.6 %collective-permute-done.1 = f32[512,512]{1,0:T(8,128)} collective-permute-done((f32[512,512]{1,0:T(8,128)}, f32[512,512]{1,0:T(8,128)}, u32[]{:S(2)}, u32[]{:S(2)}) %collective-permute-start.1) | collective-permute-done | bytes 1048608 | tf_op jit(solution)/shard_map/ppermute | solution.py:12
  21.4 1.7 fusion.34
  23.0 31.6 %all_to_all.20 = f32[8,64,512]{2,1,0:T(8,128)S(1)} all-to-all(f32[8,64,512]{2,1,0:T(8,128)S(1)} %bitcast.92), channel_id=1, replica_groups=mesh['col'=8,'y'=8,'x'=4,'core'=2] {'y'}, dimensions={0} | all-to-all | bytes 2097152 | tf_op jit(solution)/shard_map/all_to_all | solution.py:18
  54.7 7.2 %all_to_all.21 = f32[4,16,512]{2,1,0:T(8,128)S(1)} all-to-all(f32[4,16,512]{2,1,0:T(8,128)S(1)} %bitcast.93), channel_id=1, replica_groups=mesh['col'=8,'y'=8,'x'=4,'core'=2] {'x'}, dimensions={0} | all-to-all | bytes 262144 | tf_op jit(solution)/shard_map/all_to_all | solution.py:18
  61.9 7.2 %all_to_all.22 = f32[4,16,512]{2,1,0:T(8,128)S(1)} all-to-all(f32[4,16,512]{2,1,0:T(8,128)S(1)} %broadcast_in_dim.45), channel_id=1, replica_groups=mesh['col'=8,'y'=8,'x'=4,'core'=2] {'x'}, dimensions={0} | all-to-all | bytes 262144 | tf_op jit(solution)/shard_map/all_to_all | solution.py:24
  69.3 27.0 %all_to_all.23 = f32[8,64,512]{2,1,0:T(8,128)S(1)} all-to-all(f32[8,64,512]{2,1,0:T(8,128)S(1)} %broadcast_in_dim.47), channel_id=1, replica_groups=mesh['col'=8,'y'=8,'x'=4,'core'=2] {'y'}, dimensions={0} | all-to-all | bytes 2097152 | tf_op jit(solution)/shard_map/all_to_all | solution.py:24
  96.3 7.0 %collective-permute-start.2 = (f32[512,512]{1,0:T(8,128)S(1)}, f32[512,512]{1,0:T(8,128)}, u32[]{:S(2)}, u32[]{:S(2)}) collective-permute-start(f32[512,512]{1,0:T(8,128)S(1)} %bitcast.90), channel_id=1, source_target_pairs={{0,1},{1,0},{2,3},{3,2},{4,5},{5,4},{6,7},{7,6},{8,9},{9,8},{10,11... | collective-permute-start | bytes 3145736 | tf_op jit(solution)/shard_map/ppermute | solution.py:12
  103.3 1.8 fusion.67
  105.1 1.3 copy.39
  106.4 2.1 fusion.61
  108.6 1.8 fusion.28
  110.6 43.7 %while.10 = (s32[]{:T(128)}, f32[1280,128]{1,0:T(8,128)S(1)}, f32[512,512]{1,0:T(8,128)S(1)}, f32[512,512]{1,0:T(8,128)}, s32[]{:T(128)}) while((s32[]{:T(128)}, f32[1280,128]{1,0:T(8,128)S(1)}, f32[512,512]{1,0:T(8,128)S(1)}, f32[512,512]{1,0:T(8,128)}, s32[]{:T(128)}) %tuple.53), condition=%wide.region_4.5_spmd, body=%wide.region_3.4_spmd.sunk | while | flops 1614217216 | bytes 19923072 | solution.py:129
  112.7 2.1 fusion.107
  114.9 1.1 fusion.108
  119.0 2.1 fusion.107
  125.2 2.1 fusion.107
  127.3 1.0 fusion.108
  131.4 2.1 fusion.107
  137.7 2.1 fusion.107
  139.8 1.0 fusion.108
  143.9 2.1 fusion.107
  150.2 2.1 fusion.107
  152.3 1.0 fusion.108
  154.3 1.3 collective-permute-start.3
  155.6 1.3 collective-permute-start.4
  156.9 89.0 %collective-permute-done.3 = f32[1280,128]{1,0:T(8,128)S(1)} collective-permute-done((f32[1280,128]{1,0:T(8,128)S(1)}, f32[1280,128]{1,0:T(8,128)S(1)}, u32[]{:S(2)}, u32[]{:S(2)}) %collective-permute-start.3) | collective-permute-done | bytes 655392 | tf_op jit(solution)/shard_map/ppermute | solution.py:131
  248.3 1.6 fusion.31
  249.8 1.9 fusion.78
  (186 shorter events, 27.4 us)
Async XLA Ops:
  0.6 1.2 copy-start
  0.6 4.4 %copy-start.7 = (s32[1,1,2]{2,1,0:T(1,128)S(1)}, s32[1,1,2]{2,1,0:T(1,128)}, u32[]{:S(2)}) copy-start(s32[1,1,2]{2,1,0:T(1,128)} %param.15) | copy-start | bytes 28
  0.7 4.4 %copy-start.5 = (bf16[1,1,2,512,512]{4,3,2,1,0:T(8,128)(2,1)S(1)}, bf16[1,1,2,512,512]{4,3,2,1,0:T(8,128)(2,1)}, u32[]{:S(2)}) copy-start(bf16[1,1,2,512,512]{4,3,2,1,0:T(8,128)(2,1)} %param.9) | copy-start | bytes 3145732
  1.9 3.6 %copy-start.3 = (bf16[1,512,512]{2,1,0:T(8,128)(2,1)S(1)}, bf16[1,512,512]{2,1,0:T(8,128)(2,1)}, u32[]{:S(2)}) copy-start(bf16[1,512,512]{2,1,0:T(8,128)(2,1)} %param.12) | copy-start | bytes 1572868
  5.9 2.7 %copy-start.6 = (f32[1,8,512]{2,1,0:T(8,128)S(1)}, f32[1,8,512]{2,1,0:T(8,128)}, u32[]{:S(2)}) copy-start(f32[1,8,512]{2,1,0:T(8,128)} %param.13) | copy-start | bytes 49156
  10.0 11.4 %collective-permute-start.1 = (f32[512,512]{1,0:T(8,128)}, f32[512,512]{1,0:T(8,128)}, u32[]{:S(2)}, u32[]{:S(2)}) collective-permute-start(f32[512,512]{1,0:T(8,128)} %fusion.32), channel_id=1, source_target_pairs={{0,1},{1,0},{2,3},{3,2},{4,5},{5,4},{6,7},{7,6},{8,9},{9,8},{10,11... | collective-permute-start | bytes 3145736 | tf_op jit(solution)/shard_map/ppermute | solution.py:12
  96.3 14.0 %collective-permute-start.2 = (f32[512,512]{1,0:T(8,128)S(1)}, f32[512,512]{1,0:T(8,128)}, u32[]{:S(2)}, u32[]{:S(2)}) collective-permute-start(f32[512,512]{1,0:T(8,128)S(1)} %bitcast.90), channel_id=1, source_target_pairs={{0,1},{1,0},{2,3},{3,2},{4,5},{5,4},{6,7},{7,6},{8,9},{9,8},{10,11... | collective-permute-start | bytes 3145736 | tf_op jit(solution)/shard_map/ppermute | solution.py:12
  106.4 2.1 copy-start.4
  112.7 2.1 copy-start.1
  116.1 0.7 collective-permute-start
  119.0 2.1 copy-start.1
  122.3 0.7 collective-permute-start
  125.2 2.1 copy-start.1
  128.6 0.7 collective-permute-start
  131.4 2.1 copy-start.1
  134.8 0.7 collective-permute-start
  137.7 2.1 copy-start.1
  141.1 0.7 collective-permute-start
  143.9 2.1 copy-start.1
  147.3 0.7 collective-permute-start
  150.2 2.1 copy-start.1
  153.6 0.7 collective-permute-start
  154.3 91.6 %collective-permute-start.3 = (f32[1280,128]{1,0:T(8,128)S(1)}, f32[1280,128]{1,0:T(8,128)S(1)}, u32[]{:S(2)}, u32[]{:S(2)}) collective-permute-start(f32[1280,128]{1,0:T(8,128)S(1)} %get-tuple-element.24), channel_id=1, source_target_pairs={{0,1},{2,3},{4,5},{6,7},{8,9},{10,11},{12,13},{14,15},{16,17},{18,... | collective-permute-start | bytes 1966088 | tf_op jit(solution)/shard_map/ppermute | solution.py:131
  155.6 94.3 %collective-permute-start.4 = (f32[512,512]{1,0:T(8,128)}, f32[512,512]{1,0:T(8,128)}, u32[]{:S(2)}, u32[]{:S(2)}) collective-permute-start(f32[512,512]{1,0:T(8,128)} %get-tuple-element.140), channel_id=1, source_target_pairs={{0,1},{2,3},{4,5},{6,7},{8,9},{10,11},{12,13},{14,15},{16,17},{18,... | collective-permute-start | bytes 3145736 | tf_op jit(solution)/shard_map/ppermute | solution.py:130
  246.7 1.6 copy-start.2

commit v8 on v6

--- a/solution.py
+++ b/solution.py
@@ -43,31 +43,43 @@
 
 def pack(matrix):
     size = matrix.shape[0] // BLOCKS
-    return jnp.concatenate(
-        [
-            matrix[i * size : (i + 1) * size, j * size : (j + 1) * size]
-            for i in range(BLOCKS)
-            for j in range(i + 1)
-        ],
-        axis=0,
-    )
+    block = lambda i, j: matrix[i * size : (i + 1) * size, j * size : (j + 1) * size]
+    rows = lax.broadcasted_iota(jnp.int32, (size, size), 0)
+    cols = lax.broadcasted_iota(jnp.int32, (size, size), 1)
+    parts = [block(i, j) for i in range(BLOCKS) for j in range(i)]
+    diagonals = []
+    for i in range(0, BLOCKS, 2):
+        parts.append(jnp.where(rows >= cols, block(i, i), block(i + 1, i + 1).T))
+        diagonals.append(jnp.diagonal(block(i + 1, i + 1)))
+    tail = jnp.zeros((8, size), matrix.dtype).at[: len(diagonals)].set(jnp.stack(diagonals))
+    return jnp.concatenate(parts + [tail], axis=0)
 
 
 def unpack(packed, width):
     size = width // BLOCKS
+    rows = lax.broadcasted_iota(jnp.int32, (size, size), 0)
+    cols = lax.broadcasted_iota(jnp.int32, (size, size), 1)
     blocks = {}
     k = 0
     for i in range(BLOCKS):
-        for j in range(i + 1):
+        for j in range(i):
             blocks[i, j] = packed[k * size : (k + 1) * size]
             k += 1
-    rows = [
+    tail = packed[-8:]
+    for n, i in enumerate(range(0, BLOCKS, 2)):
+        folded = packed[k * size : (k + 1) * size]
+        k += 1
+        blocks[i, i] = jnp.where(rows >= cols, folded, folded.T)
+        blocks[i + 1, i + 1] = jnp.where(
+            rows > cols, folded.T, jnp.where(rows < cols, folded, tail[n][None, :])
+        )
+    rows_of = [
         jnp.concatenate(
             [blocks[i, j] if i >= j else blocks[j, i].T for j in range(BLOCKS)], axis=1
         )
         for i in range(BLOCKS)
     ]
-    return jnp.concatenate(rows, axis=0)
+    return jnp.concatenate(rows_of, axis=0)
 
 
 def symmetrize(matrix):
@@ -125,7 +137,7 @@
         )
         return lax.ppermute(pack(advanced), ("col", "core"), down)
 
-    start = jnp.zeros((BLOCKS * (BLOCKS + 1) // 2 * width // BLOCKS, width // BLOCKS), jnp.float32)
+    start = jnp.zeros((BLOCKS * BLOCKS // 2 * width // BLOCKS + 8, width // BLOCKS), jnp.float32)
     packed = lax.fori_loop(0, groups - 1, sweep, start)
     own_map = jnp.where(core == 0, chain_own, lax.ppermute(chain_own, "core", [(0, 1)]))
     shared = lax.ppermute(packed, "core", [(0, 1)])

time: 236 us -> 322 us (1.36)
  local copies, waits for them, and re-layouts: 18.3 us -> 98.9 us
  other arithmetic: 5.57 us -> 16.3 us
  waiting for transfers between devices: 91.4 us -> 83 us
    while x70 -> x71, local copies, waits for them, and re-layouts: 0.7 us -> 30.8 us
    concatenate x7 -> x14, local copies, waits for them, and re-layouts: 0.08 us -> 18.9 us  [pack(): return jnp.concatenate(parts + [tail], axis=0)]
    gather x0 -> x14, local copies, waits for them, and re-layouts: none -> 17.9 us  [pack(): diagonals.append(jnp.diagonal(block(i + 1, i + 1)))]
    ppermute x1, waiting for transfers between devices: 88.8 us -> 80.4 us  [on_device(): shared = lax.ppermute(packed, 'core', [(0, 1)])]
    slice x0 -> x8, other arithmetic: none -> 7.35 us  [unpack(): folded = packed[k * size:(k + 1) * size]]
    another operation x7 -> x14, local copies, waits for them, and re-layouts: 1.6 us -> 8.15 us
    slice x0 -> x17, local copies, waits for them, and re-layouts: none -> 5.34 us  [the longest x7 4.55 us: pack(): matrix[i * size:(i + 1) * size, j * size:(j + 1) * size]]
    slice x29 -> x15, local copies, waits for them, and re-layouts: 7.03 us -> 1.99 us  [unpack(): blocks[i, j] = packed[k * size:(k + 1) * size]]
  transfers between devices with their start and end apart: 11 -> 11, of which waited for: 2 -> 2; matrix products, arithmetic and copies ran while one was open for 4% -> 7% of each run, Pallas kernels for 0% -> 0%
where the time goes in v8:
time: 322 us; the launch traced here: 319 us
  local copies, waits for them, and re-layouts  98.9 us (31%)
  waiting for transfers between devices  83 us (26%)
  blocking collectives  55.4 us (17%)
  matrix products  38.7 us (12%)
  starting transfers between devices  22.8 us (7%)
  other arithmetic  16.3 us (5%)
    ppermute x1, waiting for transfers between devices, on_device(): shared = lax.ppermute(packed, 'core', [(0, 1)])  80.4 us
    all_to_all x2, blocking collectives, scatter_sum(): return jnp.sum(lax.all_to_all(pieces, axis, 0, 0), axis=0)  29.4 us
    while x70, local copies, waits for them, and re-layouts  28.3 us
    all_to_all x2, blocking collectives, gather_all(): gathered = lax.all_to_all(spread, axis, 0, 0)  26 us
    concatenate x14, local copies, waits for them, and re-layouts, pack(): return jnp.concatenate(parts + [tail], axis=0)  18.9 us
    gather x14, local copies, waits for them, and re-layouts, pack(): diagonals.append(jnp.diagonal(block(i + 1, i + 1)))  17.9 us
    ppermute x2, starting transfers between devices, swap_cores(): return lax.ppermute(value, 'core', [(0, 1), (1, 0)])  15.3 us
    dot_general x7, matrix products, sweep(): jnp.dot(incoming, link_wide, precision=chain)  15 us
  transfers between devices with their start and end apart: 11, of which 2 were waited for; matrix products, arithmetic and copies ran while one was open for 7% of the time, Pallas kernels for 0%

profile of v8, /device:TPU:1, one launch (start us, length us, event | category | flops | bytes accessed | tf_op | source)
XLA Modules:
  0.0 318.5 jit_solution(16914308234346983430)
XLA Ops:
  1.9 3.2 fusion.64
  5.9 2.7 fusion.29
  10.0 8.7 %collective-permute-start.1 = (f32[512,512]{1,0:T(8,128)}, f32[512,512]{1,0:T(8,128)}, u32[]{:S(2)}, u32[]{:S(2)}) collective-permute-start(f32[512,512]{1,0:T(8,128)} %fusion.32), channel_id=1, source_target_pairs={{0,1},{1,0},{2,3},{3,2},{4,5},{5,4},{6,7},{7,6},{8,9},{9,8},{10,11... | collective-permute-start | bytes 3145736 | tf_op jit(solution)/shard_map/ppermute | solution.py:12
  18.7 2.6 collective-permute-done.1
  23.0 17.2 %all_to_all.20 = f32[4,128,512]{2,1,0:T(8,128)S(1)} all-to-all(f32[4,128,512]{2,1,0:T(8,128)S(1)} %bitcast.134), channel_id=1, replica_groups=mesh['col'=8,'y'=8,'x'=4,'core'=2] {'x'}, dimensions={0} | all-to-all | bytes 2097152 | tf_op jit(solution)/shard_map/all_to_all | solution.py:18
  40.4 12.1 %all_to_all.21 = f32[8,16,512]{2,1,0:T(8,128)S(1)} all-to-all(f32[8,16,512]{2,1,0:T(8,128)S(1)} %bitcast.135), channel_id=1, replica_groups=mesh['col'=8,'y'=8,'x'=4,'core'=2] {'y'}, dimensions={0} | all-to-all | bytes 524288 | tf_op jit(solution)/shard_map/all_to_all | solution.py:18
  52.5 12.2 %all_to_all.22 = f32[8,16,512]{2,1,0:T(8,128)S(1)} all-to-all(f32[8,16,512]{2,1,0:T(8,128)S(1)} %broadcast_in_dim.94), channel_id=1, replica_groups=mesh['col'=8,'y'=8,'x'=4,'core'=2] {'y'}, dimensions={0} | all-to-all | bytes 524288 | tf_op jit(solution)/shard_map/all_to_all | solution.py:24
  64.9 13.8 %all_to_all.23 = f32[4,128,512]{2,1,0:T(8,128)S(1)} all-to-all(f32[4,128,512]{2,1,0:T(8,128)S(1)} %broadcast_in_dim.96), channel_id=1, replica_groups=mesh['col'=8,'y'=8,'x'=4,'core'=2] {'x'}, dimensions={0} | all-to-all | bytes 2097152 | tf_op jit(solution)/shard_map/all_to_all | solution.py:24
  78.7 6.6 %collective-permute-start.2 = (f32[512,512]{1,0:T(8,128)S(1)}, f32[512,512]{1,0:T(8,128)}, u32[]{:S(2)}, u32[]{:S(2)}) collective-permute-start(f32[512,512]{1,0:T(8,128)S(1)} %bitcast.132), channel_id=1, source_target_pairs={{0,1},{1,0},{2,3},{3,2},{4,5},{5,4},{6,7},{7,6},{8,9},{9,8},{10,11... | collective-permute-start | bytes 3145736 | tf_op jit(solution)/shard_map/ppermute | solution.py:12
  85.2 1.8 fusion.67
  88.4 2.1 fusion.61
  90.5 1.7 fusion.28
  92.2 2.6 copy.126
  95.1 126.3 %while.13 = (s32[]{:T(128)}, f32[1032,128]{1,0:T(8,128)S(1)}, f32[512,512]{1,0:T(8,128)S(1)}, f32[512,512]{0,1:T(8,128)}, s32[]{:T(128)}) while((s32[]{:T(128)}, f32[1032,128]{1,0:T(8,128)S(1)}, f32[512,512]{1,0:T(8,128)S(1)}, f32[512,512]{0,1:T(8,128)}, s32[]{:T(128)}) %tuple.85), condition=%wide.region_4.5_spmd, body=%wide.region_3.4_spmd.sunk | while | flops 1614463744 | bytes 22393472 | solution.py:141
  98.8 2.1 fusion.110
  110.3 2.1 copy.171
  116.8 2.1 fusion.110
  128.4 2.1 copy.171
  134.9 2.1 fusion.110
  146.4 2.1 copy.171
  152.9 2.1 fusion.110
  164.4 2.1 copy.171
  171.0 2.1 fusion.110
  182.5 2.1 copy.171
  189.0 2.1 fusion.110
  200.5 2.1 copy.171
  207.0 2.1 fusion.110
  218.6 2.1 copy.171
  224.3 80.4 %collective-permute-done.3 = f32[1032,128]{1,0:T(8,128)} collective-permute-done((f32[1032,128]{1,0:T(8,128)S(1)}, f32[1032,128]{1,0:T(8,128)}, u32[]{:S(2)}, u32[]{:S(2)}) %collective-permute-start.3) | collective-permute-done | bytes 528416 | tf_op jit(solution)/shard_map/ppermute | solution.py:143
  306.7 1.8 fusion.88
  312.8 2.3 broadcast_multiply_fusion
  316.7 1.9 fusion.79
  (335 shorter events, 111.9 us)
Async XLA Ops:
  0.6 1.2 copy-start
  0.6 4.4 %copy-start.11 = (s32[1,1,2]{2,1,0:T(1,128)S(1)}, s32[1,1,2]{2,1,0:T(1,128)}, u32[]{:S(2)}) copy-start(s32[1,1,2]{2,1,0:T(1,128)} %param.17) | copy-start | bytes 28
  0.7 4.4 %copy-start.8 = (bf16[1,1,2,512,512]{4,3,2,1,0:T(8,128)(2,1)S(1)}, bf16[1,1,2,512,512]{4,3,2,1,0:T(8,128)(2,1)}, u32[]{:S(2)}) copy-start(bf16[1,1,2,512,512]{4,3,2,1,0:T(8,128)(2,1)} %param.11) | copy-start | bytes 3145732
  1.9 3.6 %copy-start.5 = (bf16[1,512,512]{2,1,0:T(8,128)(2,1)S(1)}, bf16[1,512,512]{2,1,0:T(8,128)(2,1)}, u32[]{:S(2)}) copy-start(bf16[1,512,512]{2,1,0:T(8,128)(2,1)} %param.14) | copy-start | bytes 1572868
  5.9 2.7 copy-start.10
  10.0 11.4 %collective-permute-start.1 = (f32[512,512]{1,0:T(8,128)}, f32[512,512]{1,0:T(8,128)}, u32[]{:S(2)}, u32[]{:S(2)}) collective-permute-start(f32[512,512]{1,0:T(8,128)} %fusion.32), channel_id=1, source_target_pairs={{0,1},{1,0},{2,3},{3,2},{4,5},{5,4},{6,7},{7,6},{8,9},{9,8},{10,11... | collective-permute-start | bytes 3145736 | tf_op jit(solution)/shard_map/ppermute | solution.py:12
  78.7 9.7 %copy-start.2 = (f32[4,128,512]{2,1,0:T(8,128)}, f32[4,128,512]{2,1,0:T(8,128)S(1)}, u32[]{:S(2)}) copy-start(f32[4,128,512]{2,1,0:T(8,128)S(1)} %all_to_all.23) | copy-start | bytes 3145732
  78.7 16.1 %collective-permute-start.2 = (f32[512,512]{1,0:T(8,128)S(1)}, f32[512,512]{1,0:T(8,128)}, u32[]{:S(2)}, u32[]{:S(2)}) collective-permute-start(f32[512,512]{1,0:T(8,128)S(1)} %bitcast.132), channel_id=1, source_target_pairs={{0,1},{1,0},{2,3},{3,2},{4,5},{5,4},{6,7},{7,6},{8,9},{9,8},{10,11... | collective-permute-start | bytes 3145736 | tf_op jit(solution)/shard_map/ppermute | solution.py:12
  88.4 2.1 copy-start.6
  90.5 4.3 %copy-start.3 = (f32[4,128,512]{2,1,0:T(8,128)S(1)}, f32[4,128,512]{2,1,0:T(8,128)}, u32[]{:S(2)}) copy-start(f32[4,128,512]{2,1,0:T(8,128)} %copy-done.2) | copy-start | bytes 3145732
  98.8 2.2 copy-start.1
  112.4 0.7 collective-permute-start
  116.8 2.2 copy-start.1
  130.4 0.7 collective-permute-start
  134.9 2.2 copy-start.1
  148.5 0.7 collective-permute-start
  152.9 2.2 copy-start.1
  166.5 0.7 collective-permute-start
  170.9 2.2 copy-start.1
  184.6 0.7 collective-permute-start
  189.0 2.2 copy-start.1
  202.6 0.7 collective-permute-start
  207.0 2.2 copy-start.1
  220.6 0.7 collective-permute-start
  221.3 83.3 %collective-permute-start.3 = (f32[1032,128]{1,0:T(8,128)S(1)}, f32[1032,128]{1,0:T(8,128)}, u32[]{:S(2)}, u32[]{:S(2)}) collective-permute-start(f32[1032,128]{1,0:T(8,128)S(1)} %get-tuple-element.68), channel_id=1, source_target_pairs={{0,1},{2,3},{4,5},{6,7},{8,9},{10,11},{12,13},{14,15},{16,17},{18,... | collective-permute-start | bytes 1585160 | tf_op jit(solution)/shard_map/ppermute | solution.py:143
  222.8 93.9 %collective-permute-start.4 = (f32[512,512]{1,0:T(8,128)}, f32[512,512]{1,0:T(8,128)}, u32[]{:S(2)}, u32[]{:S(2)}) collective-permute-start(f32[512,512]{1,0:T(8,128)} %fusion.28), channel_id=1, source_target_pairs={{0,1},{2,3},{4,5},{6,7},{8,9},{10,11},{12,13},{14,15},{16,17},{18,... | collective-permute-start | bytes 3145736 | tf_op jit(solution)/shard_map/ppermute | solution.py:142
  305.8 0.8 copy-start.7
  308.5 4.3 %copy-start.9 = (f32[128,128]{1,0:T(8,128)}, f32[128,128]{1,0:T(8,128)S(1)}, u32[]{:S(2)}) copy-start(f32[128,128]{1,0:T(8,128)S(1)} %get-tuple-element.131) | copy-start | bytes 196612
  312.8 2.3 copy-start.4
